TPU v7x, 512 devices: a whole 4x4x16 slice. The times are simulated.
512 devices in a mesh: grp: 8 (over z_lo, core), spec: 64 (over z_hi, x, y).
Axes of the slice: x: 4, y: 4, z: 16 (z_hi: 4, z_lo: 4; z = z_hi * 4 + z_lo), core: 2. Of those that a mesh axis runs over, the one named last changes fastest.
Arguments:
- queries: bfloat16 [262144, 1024], P(('grp', 'spec')), may hold values from -6 to 6
- out_grad: bfloat16 [262144, 1024], P(('grp', 'spec')), may hold values from -48 to 48
- spec_keys: bfloat16 [512, 192, 1024], P(('grp', 'spec')), may hold values from -6 to 6
- spec_values: bfloat16 [512, 192, 1024], P(('grp', 'spec')), may hold values from -6 to 6
- owner_of: int32 [32768, 1], P(('grp', 'spec')), may hold values from 0 to 63; in each aligned block of 64 rows (0 to 63, 64 to 127, ...) at most 2 rows name the same one
- query_gain: float32 [1024], replicated, may hold values from 0.5 to 1.5
Outputs:
- query_grad: bfloat16 [262144, 1024], P(('grp', 'spec'))
- key_grad: bfloat16 [512, 192, 1024], P(('grp', 'spec'))
- value_grad: bfloat16 [512, 192, 1024], P(('grp', 'spec'))
- gain_grad: float32 [1024], replicated
Inputs may be any that keep to these rules, and one draw needn't show every extreme that they name: `owner_of`: among the candidates of one device, at most 2 name the same spec.
All inputs are finite; a program needn't handle non-finite values.
Results may differ from a plain program's by a relative error of at most 0.012.
The roundings to bfloat16 on the way count: a program that leaves them out, or rounds other values in their place, can miss the bound.
Values may be sent and summed in bfloat16 or wider, within the bound.
No kernel may reach another device: no remote copies, remote signals or barrier semaphores. Data moves between devices by JAX's collectives and lax.ppermute only.
A program may use at most 64 MiB of HBM per device.

v0:
```python
import math

import jax
import jax.numpy as jnp
from jax import lax
from jax.sharding import PartitionSpec as P

HEADS = 8
HEAD_DIM = 128
CAP = 2


def gain_reduce(partial_value):
    return lax.psum(partial_value, ("grp", "spec"))


def send_back(going_back):
    return lax.all_to_all(going_back, "spec", split_axis=0, concat_axis=0, tiled=True)


def attend_backward(recv_rows, recv_grads, keys_here, values_here, query_gain):
    total_rows, width = recv_rows.shape
    head_dim = width // HEADS
    inv_root = 1.0 / math.sqrt(HEAD_DIM)
    gained = (recv_rows.astype(jnp.float32) * query_gain).astype(jnp.bfloat16)
    q_heads = gained.reshape(total_rows, HEADS, head_dim).transpose(1, 0, 2)
    g_heads = recv_grads.reshape(total_rows, HEADS, head_dim).transpose(1, 0, 2)
    key_count = keys_here.shape[0]
    k_heads = keys_here.reshape(key_count, HEADS, head_dim).transpose(1, 0, 2)
    v_heads = values_here.reshape(key_count, HEADS, head_dim).transpose(1, 0, 2)

    def one_head(pieces):
        q_head, g_head, k_head, v_head = pieces
        scores = (
            lax.dot_general(
                q_head, k_head, (((1,), (1,)), ((), ())), preferred_element_type=jnp.float32
            )
            * inv_root
        )
        top = jnp.max(scores, axis=1, keepdims=True)
        expo = jnp.exp(scores - top)
        probs = expo / jnp.sum(expo, axis=1, keepdims=True)
        probs_b = probs.astype(jnp.bfloat16)
        attended = jnp.dot(probs_b, v_head, preferred_element_type=jnp.float32)
        delta = jnp.sum(g_head.astype(jnp.float32) * attended, axis=1, keepdims=True)
        dprobs = lax.dot_general(
            g_head, v_head, (((1,), (1,)), ((), ())), preferred_element_type=jnp.float32
        )
        dscores = (probs * (dprobs - delta)).astype(jnp.bfloat16)
        q_grad = jnp.dot(dscores, k_head, preferred_element_type=jnp.float32) * inv_root
        k_grad = (
            lax.dot_general(
                dscores, q_head, (((0,), (0,)), ((), ())), preferred_element_type=jnp.float32
            )
            * inv_root
        )
        v_grad = lax.dot_general(
            probs_b, g_head, (((0,), (0,)), ((), ())), preferred_element_type=jnp.float32
        )
        return (q_grad, k_grad.astype(jnp.bfloat16), v_grad.astype(jnp.bfloat16))

    q_grads, k_grads, v_grads = lax.map(one_head, (q_heads, g_heads, k_heads, v_heads))
    gained_grad = q_grads.transpose(1, 0, 2).reshape(total_rows, width)
    key_grad = k_grads.transpose(1, 0, 2).reshape(key_count, width)
    value_grad = v_grads.transpose(1, 0, 2).reshape(key_count, width)
    return (gained_grad, key_grad, value_grad)


def shards(queries, out_grad, spec_keys, spec_values, owner_of, query_gain):
    peers = lax.axis_size("spec")
    cand_count = owner_of.shape[0]
    width = queries.shape[1]
    qtok_here = queries.shape[0] // cand_count
    slot_count = peers * CAP
    target = owner_of[:, 0]
    onehot = (target[:, None] == jnp.arange(peers, dtype=jnp.int32)[None, :]).astype(jnp.int32)
    earlier = jnp.cumsum(onehot, axis=0) - onehot
    position = jnp.sum(earlier * onehot, axis=1)
    slot_index = target * CAP + position
    placing = (jnp.arange(slot_count, dtype=jnp.int32)[:, None] == slot_index[None, :]).astype(
        jnp.bfloat16
    )
    flat_queries = queries.reshape(cand_count, qtok_here * width)
    flat_grads = out_grad.reshape(cand_count, qtok_here * width)
    send_queries = jnp.dot(placing, flat_queries, preferred_element_type=jnp.float32).astype(
        jnp.bfloat16
    )
    send_grads = jnp.dot(placing, flat_grads, preferred_element_type=jnp.float32).astype(
        jnp.bfloat16
    )
    recv_queries, recv_grads = (
        lax.all_to_all(send_queries, "spec", split_axis=0, concat_axis=0, tiled=True),
        lax.all_to_all(send_grads, "spec", split_axis=0, concat_axis=0, tiled=True),
    )
    recv_rows = recv_queries.reshape(slot_count * qtok_here, width)
    recv_cotan = recv_grads.reshape(slot_count * qtok_here, width)
    gained_grad, key_grad, value_grad = attend_backward(
        recv_rows, recv_cotan, spec_keys[0], spec_values[0], query_gain
    )
    partial_value = jnp.sum(recv_rows.astype(jnp.float32) * gained_grad, axis=0)
    going_back = (
        (gained_grad * query_gain).astype(jnp.bfloat16).reshape(slot_count, qtok_here * width)
    )
    came_back = send_back(going_back)
    gain_grad = gain_reduce(partial_value)
    home_grads = jnp.dot(placing.T, came_back, preferred_element_type=jnp.float32).astype(
        jnp.bfloat16
    )
    query_grad = home_grads.reshape(cand_count * qtok_here, width)
    return (query_grad, key_grad[None], value_grad[None], gain_grad)


def solution(mesh):
    return jax.shard_map(
        shards,
        mesh=mesh,
        in_specs=(
            P(("grp", "spec"), None),
            P(("grp", "spec"), None),
            P(("grp", "spec"), None, None),
            P(("grp", "spec"), None, None),
            P(("grp", "spec"), None),
            P(),
        ),
        out_specs=(
            P(("grp", "spec"), None),
            P(("grp", "spec"), None, None),
            P(("grp", "spec"), None, None),
            P(),
        ),
        check_vma=False,
    )
```

profile of v0, /device:TPU:1, one launch (start us, length us, event | category | flops | bytes accessed | tf_op | source)
XLA Modules:
  0.0 597.1 jit_solution(2373674755203871809)
XLA Ops:
  5.2 2.7 all_to_all.20
  7.9 21.7 %all-to-all-start.1 = ((bf16[64,2,8192]{2,1,0:T(2,128)(2,1)}), bf16[64,2,8192]{2,1,0:T(2,128)(2,1)S(1)}, u32[]{:S(2)}, u32[]{:S(2)}) async-start(bf16[64,2,8192]{2,1,0:T(2,128)(2,1)} %all_to_all.20), calls=%async_computation.1 | async-start | bytes 4194304 | tf_op jit(solution)/shard_map/all_to_all | solution.py:93
  31.2 2.0 convolution_convert_fusion.2
  33.2 4.4 all_to_all.18
  37.6 81.7 %all-to-all-done.1 = bf16[64,2,8192]{2,1,0:T(2,128)(2,1)S(1)} async-done(((bf16[64,2,8192]{2,1,0:T(2,128)(2,1)}), bf16[64,2,8192]{2,1,0:T(2,128)(2,1)S(1)}, u32[]{:S(2)}, u32[]{:S(2)}) %all-to-all-start.1) | async-done | bytes 2097184 | tf_op jit(solution)/shard_map/all_to_all | solution.py:93
  120.6 17.9 %all-to-all-start = ((bf16[64,2,8192]{2,1,0:T(2,128)(2,1)}), bf16[64,2,8192]{2,1,0:T(2,128)(2,1)S(1)}, u32[]{:S(2)}, u32[]{:S(2)}) async-start(bf16[64,2,8192]{2,1,0:T(2,128)(2,1)} %all_to_all.18), calls=%async_computation | async-start | bytes 4194304 | tf_op jit(solution)/shard_map/all_to_all | solution.py:92
  138.9 4.5 reshape_reshape.3
  143.4 4.1 copy.14
  147.6 87.7 %all-to-all-done = bf16[64,2,8192]{2,1,0:T(2,128)(2,1)S(1)} async-done(((bf16[64,2,8192]{2,1,0:T(2,128)(2,1)}), bf16[64,2,8192]{2,1,0:T(2,128)(2,1)S(1)}, u32[]{:S(2)}, u32[]{:S(2)}) %all-to-all-start) | async-done | bytes 2097184 | tf_op jit(solution)/shard_map/all_to_all | solution.py:92
  235.2 3.0 reshape.66
  238.3 2.4 fusion.33
  241.0 167.4 %while.14 = (s32[]{:T(128)}, f32[8,1024,128]{2,0,1:T(8,128)}, bf16[8,192,128]{2,1,0:T(8,128)(2,1)}, bf16[8,192,128]{2,1,0:T(8,128)(2,1)}, bf16[8,1024,128]{2,1,0...) while((s32[]{:T(128)}, f32[8,1024,128]{2,0,1:T(8,128)}, ...), condition=%wide.region_6.7_spmd, body=%wide.region_2.6_spmd.sunk | while | flops 304944128 | bytes 8725621 | solution.py:62
  244.0 1.8 fusion.79
  247.1 14.8 %dynamic_update_slice.18 = f32[8,1024,128]{2,0,1:T(8,128)} dynamic-update-slice(f32[8,1024,128]{2,0,1:T(8,128)} %get-tuple-element.141, f32[1,1024,128]{2,0,1:T(1,128)S(1)} %bitcast.101, s32[]{:T(128)S(6)} %copy.34, s32[]{:T(128)} %constant.34.clone.1..sunk, s32[]{:T(128)} %constant.34.clone.1..sunk) | dynamic-update-slice | bytes 1048580 | tf_op jit(solution)/shard_map/while/body/jit(dynamic_update_index_in_dim)/dynamic_update_slice | solution.py:62
  264.9 1.8 fusion.79
  268.0 14.8 %dynamic_update_slice.18 = f32[8,1024,128]{2,0,1:T(8,128)} dynamic-update-slice(f32[8,1024,128]{2,0,1:T(8,128)} %get-tuple-element.141, f32[1,1024,128]{2,0,1:T(1,128)S(1)} %bitcast.101, s32[]{:T(128)S(6)} %copy.34, s32[]{:T(128)} %constant.34.clone.1..sunk, s32[]{:T(128)} %constant.34.clone.1..sunk) | dynamic-update-slice | bytes 1048580 | tf_op jit(solution)/shard_map/while/body/jit(dynamic_update_index_in_dim)/dynamic_update_slice | solution.py:62
  285.9 1.8 fusion.79
  288.9 14.8 %dynamic_update_slice.18 = f32[8,1024,128]{2,0,1:T(8,128)} dynamic-update-slice(f32[8,1024,128]{2,0,1:T(8,128)} %get-tuple-element.141, f32[1,1024,128]{2,0,1:T(1,128)S(1)} %bitcast.101, s32[]{:T(128)S(6)} %copy.34, s32[]{:T(128)} %constant.34.clone.1..sunk, s32[]{:T(128)} %constant.34.clone.1..sunk) | dynamic-update-slice | bytes 1048580 | tf_op jit(solution)/shard_map/while/body/jit(dynamic_update_index_in_dim)/dynamic_update_slice | solution.py:62
  309.9 14.8 %dynamic_update_slice.18 = f32[8,1024,128]{2,0,1:T(8,128)} dynamic-update-slice(f32[8,1024,128]{2,0,1:T(8,128)} %get-tuple-element.141, f32[1,1024,128]{2,0,1:T(1,128)S(1)} %bitcast.101, s32[]{:T(128)S(6)} %copy.34, s32[]{:T(128)} %constant.34.clone.1..sunk, s32[]{:T(128)} %constant.34.clone.1..sunk) | dynamic-update-slice | bytes 1048580 | tf_op jit(solution)/shard_map/while/body/jit(dynamic_update_index_in_dim)/dynamic_update_slice | solution.py:62
  327.7 1.8 fusion.79
  330.8 14.8 %dynamic_update_slice.18 = f32[8,1024,128]{2,0,1:T(8,128)} dynamic-update-slice(f32[8,1024,128]{2,0,1:T(8,128)} %get-tuple-element.141, f32[1,1024,128]{2,0,1:T(1,128)S(1)} %bitcast.101, s32[]{:T(128)S(6)} %copy.34, s32[]{:T(128)} %constant.34.clone.1..sunk, s32[]{:T(128)} %constant.34.clone.1..sunk) | dynamic-update-slice | bytes 1048580 | tf_op jit(solution)/shard_map/while/body/jit(dynamic_update_index_in_dim)/dynamic_update_slice | solution.py:62
  351.7 14.8 %dynamic_update_slice.18 = f32[8,1024,128]{2,0,1:T(8,128)} dynamic-update-slice(f32[8,1024,128]{2,0,1:T(8,128)} %get-tuple-element.141, f32[1,1024,128]{2,0,1:T(1,128)S(1)} %bitcast.101, s32[]{:T(128)S(6)} %copy.34, s32[]{:T(128)} %constant.34.clone.1..sunk, s32[]{:T(128)} %constant.34.clone.1..sunk) | dynamic-update-slice | bytes 1048580 | tf_op jit(solution)/shard_map/while/body/jit(dynamic_update_index_in_dim)/dynamic_update_slice | solution.py:62
  369.5 1.8 fusion.79
  372.6 14.8 %dynamic_update_slice.18 = f32[8,1024,128]{2,0,1:T(8,128)} dynamic-update-slice(f32[8,1024,128]{2,0,1:T(8,128)} %get-tuple-element.141, f32[1,1024,128]{2,0,1:T(1,128)S(1)} %bitcast.101, s32[]{:T(128)S(6)} %copy.34, s32[]{:T(128)} %constant.34.clone.1..sunk, s32[]{:T(128)} %constant.34.clone.1..sunk) | dynamic-update-slice | bytes 1048580 | tf_op jit(solution)/shard_map/while/body/jit(dynamic_update_index_in_dim)/dynamic_update_slice | solution.py:62
  393.6 14.8 %dynamic_update_slice.18 = f32[8,1024,128]{2,0,1:T(8,128)} dynamic-update-slice(f32[8,1024,128]{2,0,1:T(8,128)} %get-tuple-element.141, f32[1,1024,128]{2,0,1:T(1,128)S(1)} %bitcast.101, s32[]{:T(128)S(6)} %copy.34, s32[]{:T(128)} %constant.34.clone.1..sunk, s32[]{:T(128)} %constant.34.clone.1..sunk) | dynamic-update-slice | bytes 1048580 | tf_op jit(solution)/shard_map/while/body/jit(dynamic_update_index_in_dim)/dynamic_update_slice | solution.py:62
  408.4 5.8 reshape.64
  414.2 5.5 multiply_convert_fusion
  419.7 13.1 %all-to-all-start.2 = ((bf16[64,2,8192]{2,1,0:T(2,128)(2,1)}), bf16[64,2,8192]{2,1,0:T(2,128)(2,1)S(1)}, u32[]{:S(2)}, u32[]{:S(2)}) async-start(bf16[64,2,8192]{2,1,0:T(2,128)(2,1)} %multiply_convert_fusion), calls=%async_computation.2 | async-start | bytes 4194304 | tf_op jit(solution)/shard_map/all_to_all | solution.py:18
  437.1 4.5 multiply_reduce_fusion
  441.7 149.8 %psum.7 = f32[1024]{0:T(1024)} all-reduce(f32[1024]{0:T(1024)S(1)} %bitcast.109), channel_id=1, replica_groups=mesh['grp'=8,'spec'=64] {'grp','spec'}, use_global_device_ids=true, to_apply=%region_8.9 | all-reduce | flops 1024 | bytes 8192 | tf_op jit(solution)/shard_map/psum | solution.py:14
  591.5 2.2 all_to_all.23
  593.7 2.1 convolution_convert_fusion.3
  (90 shorter events, 52.8 us)
Async XLA Ops:
  7.9 111.4 %all-to-all-start.1 = ((bf16[64,2,8192]{2,1,0:T(2,128)(2,1)}), bf16[64,2,8192]{2,1,0:T(2,128)(2,1)S(1)}, u32[]{:S(2)}, u32[]{:S(2)}) async-start(bf16[64,2,8192]{2,1,0:T(2,128)(2,1)} %all_to_all.20), calls=%async_computation.1 | async-start | bytes 4194304 | tf_op jit(solution)/shard_map/all_to_all | solution.py:93
  37.6 101.0 %copy-start.3 = (f32[1024]{0:T(1024)S(1)}, f32[1024]{0:T(1024)}, u32[]{:S(2)}) copy-start(f32[1024]{0:T(1024)} %param.13) | copy-start | bytes 12292
  37.6 101.0 %copy-start.1 = (bf16[1,192,1024]{2,1,0:T(8,128)(2,1)S(1)}, bf16[1,192,1024]{2,1,0:T(8,128)(2,1)}, u32[]{:S(2)}) copy-start(bf16[1,192,1024]{2,1,0:T(8,128)(2,1)} %param.10) | copy-start | bytes 1179652
  37.6 101.1 %copy-start.2 = (bf16[1,192,1024]{2,1,0:T(8,128)(2,1)S(1)}, bf16[1,192,1024]{2,1,0:T(8,128)(2,1)}, u32[]{:S(2)}) copy-start(bf16[1,192,1024]{2,1,0:T(8,128)(2,1)} %param.11) | copy-start | bytes 1179652
  119.3 1.3 copy-start
  120.6 114.7 %all-to-all-start = ((bf16[64,2,8192]{2,1,0:T(2,128)(2,1)}), bf16[64,2,8192]{2,1,0:T(2,128)(2,1)S(1)}, u32[]{:S(2)}, u32[]{:S(2)}) async-start(bf16[64,2,8192]{2,1,0:T(2,128)(2,1)} %all_to_all.18), calls=%async_computation | async-start | bytes 4194304 | tf_op jit(solution)/shard_map/all_to_all | solution.py:92
  419.7 171.8 %all-to-all-start.2 = ((bf16[64,2,8192]{2,1,0:T(2,128)(2,1)}), bf16[64,2,8192]{2,1,0:T(2,128)(2,1)S(1)}, u32[]{:S(2)}, u32[]{:S(2)}) async-start(bf16[64,2,8192]{2,1,0:T(2,128)(2,1)} %multiply_convert_fusion), calls=%async_computation.2 | async-start | bytes 4194304 | tf_op jit(solution)/shard_map/all_to_all | solution.py:18
where the time goes:
time: 601 us; the launch traced here: 597 us
  waiting for transfers between devices  169 us (28%)
  local copies, waits for them, and re-layouts  156 us (26%)
  blocking collectives  150 us (25%)
  starting transfers between devices  52.7 us (9%)
  matrix products  51.2 us (9%)
  other arithmetic  16.9 us (3%)
    psum x1, blocking collectives, gain_reduce(): return lax.psum(partial_value, ('grp', 'spec'))  150 us
    dynamic_update_slice x8, local copies, waits for them, and re-layouts, attend_backward(): lax.map(one_head, (q_heads, g_heads, k_heads, v_heads))  119 us
    all_to_all x1, waiting for transfers between devices, shards(): lax.all_to_all(send_queries, 'spec', split_axis=0, concat_axis=0, tiled=T...  87.7 us
    all_to_all x1, waiting for transfers between devices, shards(): lax.all_to_all(send_grads, 'spec', split_axis=0, concat_axis=0, tiled=True)  81.7 us
    all_to_all x1, starting transfers between devices, shards(): lax.all_to_all(send_grads, 'spec', split_axis=0, concat_axis=0, tiled=True)  21.7 us
    all_to_all x1, starting transfers between devices, shards(): lax.all_to_all(send_queries, 'spec', split_axis=0, concat_axis=0, tiled=T...  17.9 us
    dot_general x8, matrix products, one_head(): lax.dot_general(probs_b, g_head, (((0,), (0,)), ((), ())), preferred_elem...  14.8 us
    all_to_all x1, starting transfers between devices, send_back(): lax.all_to_all(going_back, 'spec', split_axis=0, concat_axis=0, tiled=True)  13.1 us
  transfers between devices with their start and end apart: 3, of which 2 were waited for; matrix products, arithmetic and copies ran while one was open for 4% of the time, Pallas kernels for 0%

commit v1 on v0

v1 whole, which is shorter than its diff:
```python
import math

import jax
import jax.numpy as jnp
from jax import lax
from jax.sharding import PartitionSpec as P

HEADS = 8
HEAD_DIM = 128
CAP = 2


def attend_backward(recv_rows, recv_grads, keys_here, values_here, query_gain):
    total_rows, width = recv_rows.shape
    head_dim = width // HEADS
    inv_root = 1.0 / math.sqrt(HEAD_DIM)
    gained = (recv_rows.astype(jnp.float32) * query_gain).astype(jnp.bfloat16)
    key_count = keys_here.shape[0]
    q_heads = gained.reshape(total_rows, HEADS, head_dim)
    g_heads = recv_grads.reshape(total_rows, HEADS, head_dim)
    k_heads = keys_here.reshape(key_count, HEADS, head_dim)
    v_heads = values_here.reshape(key_count, HEADS, head_dim)
    f32 = jnp.float32
    scores = jnp.einsum("rhd,khd->hrk", q_heads, k_heads, preferred_element_type=f32) * inv_root
    top = jnp.max(scores, axis=2, keepdims=True)
    expo = jnp.exp(scores - top)
    probs = expo / jnp.sum(expo, axis=2, keepdims=True)
    probs_b = probs.astype(jnp.bfloat16)
    attended = jnp.einsum("hrk,khd->rhd", probs_b, v_heads, preferred_element_type=f32)
    delta = jnp.sum(g_heads.astype(f32) * attended, axis=2)
    dprobs = jnp.einsum("rhd,khd->hrk", g_heads, v_heads, preferred_element_type=f32)
    dscores = (probs * (dprobs - delta.T[:, :, None])).astype(jnp.bfloat16)
    q_grad = jnp.einsum("hrk,khd->rhd", dscores, k_heads, preferred_element_type=f32) * inv_root
    k_grad = jnp.einsum("hrk,rhd->khd", dscores, q_heads, preferred_element_type=f32) * inv_root
    v_grad = jnp.einsum("hrk,rhd->khd", probs_b, g_heads, preferred_element_type=f32)
    gained_grad = q_grad.reshape(total_rows, width)
    return (gained_grad, k_grad.reshape(key_count, width), v_grad.reshape(key_count, width))


def shards(queries, out_grad, spec_keys, spec_values, owner_of, query_gain):
    peers = lax.axis_size("spec")
    cand_count = owner_of.shape[0]
    width = queries.shape[1]
    qtok_here = queries.shape[0] // cand_count
    target = owner_of[:, 0]
    onehot = (target[:, None] == jnp.arange(peers, dtype=jnp.int32)[None, :]).astype(jnp.int32)
    earlier = jnp.cumsum(onehot, axis=0) - onehot
    position = jnp.sum(earlier * onehot, axis=1)
    flat_both = jnp.concatenate(
        [queries.reshape(cand_count, qtok_here * width), out_grad.reshape(cand_count, qtok_here * width)],
        axis=1,
    )
    keys_here, values_here = spec_keys[0], spec_values[0]
    home_grads = None
    key_acc = None
    value_acc = None
    gain_acc = None
    for slot in range(CAP):
        placing = (
            (jnp.arange(peers, dtype=jnp.int32)[:, None] == target[None, :])
            & (position[None, :] == slot)
        ).astype(jnp.bfloat16)
        send_both = jnp.dot(placing, flat_both, preferred_element_type=jnp.float32).astype(
            jnp.bfloat16
        )
        recv_both = lax.all_to_all(send_both, "spec", split_axis=0, concat_axis=0, tiled=True)
        recv_rows = recv_both[:, : qtok_here * width].reshape(peers * qtok_here, width)
        recv_cotan = recv_both[:, qtok_here * width :].reshape(peers * qtok_here, width)
        gained_grad, key_part, value_part = attend_backward(
            recv_rows, recv_cotan, keys_here, values_here, query_gain
        )
        gain_part = jnp.sum(recv_rows.astype(jnp.float32) * gained_grad, axis=0)
        going_back = (
            (gained_grad * query_gain).astype(jnp.bfloat16).reshape(peers, qtok_here * width)
        )
        came_back = lax.all_to_all(going_back, "spec", split_axis=0, concat_axis=0, tiled=True)
        home_part = jnp.dot(placing.T, came_back, preferred_element_type=jnp.float32)
        if home_grads is None:
            home_grads, key_acc, value_acc, gain_acc = home_part, key_part, value_part, gain_part
        else:
            home_grads = home_grads + home_part
            key_acc = key_acc + key_part
            value_acc = value_acc + value_part
            gain_acc = gain_acc + gain_part
    gain_grad = lax.psum(gain_acc, ("grp", "spec"))
    query_grad = home_grads.astype(jnp.bfloat16).reshape(cand_count * qtok_here, width)
    key_grad = key_acc.astype(jnp.bfloat16)
    value_grad = value_acc.astype(jnp.bfloat16)
    return (query_grad, key_grad[None], value_grad[None], gain_grad)


def solution(mesh):
    return jax.shard_map(
        shards,
        mesh=mesh,
        in_specs=(
            P(("grp", "spec"), None),
            P(("grp", "spec"), None),
            P(("grp", "spec"), None, None),
            P(("grp", "spec"), None, None),
            P(("grp", "spec"), None),
            P(),
        ),
        out_specs=(
            P(("grp", "spec"), None),
            P(("grp", "spec"), None, None),
            P(("grp", "spec"), None, None),
            P(),
        ),
        check_vma=False,
    )
```

time: 601 us -> 537 us (0.89)
  local copies, waits for them, and re-layouts: 156 us -> 90.9 us
  blocking collectives: 150 us -> 113 us
  waiting for transfers between devices: 169 us -> 201 us
  matrix products: 51.2 us -> 28.5 us
  other arithmetic: 16.9 us -> 32.1 us
  starting transfers between devices: 52.7 us -> 62.8 us
    dynamic_update_slice x8 -> x0, local copies, waits for them, and re-layouts: 119 us -> none  [attend_backward(): lax.map(one_head, (q_heads, g_heads, k_heads, v_heads))]
    unnamed x12 -> x73, local copies, waits for them, and re-layouts: 1.44 us -> 58.2 us
    psum x1, blocking collectives: 150 us -> 113 us  [shards(): gain_grad = lax.psum(gain_acc, ('grp', 'spec'))]
    all_to_all x3 -> x4, waiting for transfers between devices: 169 us -> 201 us  [the longest x2 155 us: shards(): lax.all_to_all(send_both, 'spec', split_axis=0, concat_axis=0, tiled=True)]
    dot_general x50 -> x14, matrix products: 49.1 us -> 22.4 us  [the longest x2 5.9 us: attend_backward(): jnp.einsum('hrk,khd->rhd', dscores, k_heads, preferred_element_type=f32)]
    all_to_all x3 -> x4, starting transfers between devices: 52.7 us -> 62.8 us  [the longest x2 41.1 us: shards(): lax.all_to_all(send_both, 'spec', split_axis=0, concat_axis=0, tiled=True)]
    all_to_all x3 -> x1, local copies, waits for them, and re-layouts: 9.28 us -> 0.54 us  [shards(): lax.all_to_all(send_both, 'spec', split_axis=0, concat_axis=0, tiled=True)]
    all_to_all x0 -> x2, other arithmetic: none -> 8.3 us  [shards(): lax.all_to_all(send_both, 'spec', split_axis=0, concat_axis=0, tiled=True)]
  transfers between devices with their start and end apart: 3 -> 4, of which waited for: 2 -> 3; matrix products, arithmetic and copies ran while one was open for 4% -> 10% of each run, Pallas kernels for 0% -> 0%
where the time goes in v1:
time: 537 us; the launch traced here: 529 us
  waiting for transfers between devices  201 us (37%)
  blocking collectives  113 us (21%)
  local copies, waits for them, and re-layouts  90.9 us (17%)
  starting transfers between devices  62.8 us (12%)
  other arithmetic  32.1 us (6%)
  matrix products  28.5 us (5%)
    all_to_all x2, waiting for transfers between devices, shards(): lax.all_to_all(send_both, 'spec', split_axis=0, concat_axis=0, tiled=True)  155 us
    psum x1, blocking collectives, shards(): gain_grad = lax.psum(gain_acc, ('grp', 'spec'))  113 us
    unnamed x73, local copies, waits for them, and re-layouts  58.2 us
    all_to_all x2, waiting for transfers between devices, shards(): lax.all_to_all(going_back, 'spec', split_axis=0, concat_axis=0, tiled=True)  46.2 us
    all_to_all x2, starting transfers between devices, shards(): lax.all_to_all(send_both, 'spec', split_axis=0, concat_axis=0, tiled=True)  41.1 us
    all_to_all x2, starting transfers between devices, shards(): lax.all_to_all(going_back, 'spec', split_axis=0, concat_axis=0, tiled=True)  21.6 us
  transfers between devices with their start and end apart: 4, of which 3 were waited for; matrix products, arithmetic and copies ran while one was open for 10% of the time, Pallas kernels for 0%

profile of v1, /device:TPU:1, one launch (start us, length us, event | category | flops | bytes accessed | tf_op | source)
XLA Modules:
  0.0 529.3 jit_solution(479831627291355458)
XLA Ops:
  8.2 4.5 reduce.3
  12.7 4.5 reshape.214
  17.2 22.0 %all-to-all-start = ((bf16[64,2,8192]{2,1,0:T(2,128)(2,1)}), bf16[64,2,8192]{2,1,0:T(2,128)(2,1)}, u32[]{:S(2)}, u32[]{:S(2)}) async-start(bf16[64,2,8192]{2,1,0:T(2,128)(2,1)} %reshape.214), calls=%async_computation | async-start | bytes 4194304 | tf_op jit(solution)/shard_map/all_to_all | solution.py:66
  41.2 3.8 reduce.2
  45.0 2.8 reshape.218
  47.8 80.7 %all-to-all-done = bf16[64,2,8192]{2,1,0:T(2,128)(2,1)} async-done(((bf16[64,2,8192]{2,1,0:T(2,128)(2,1)}), bf16[64,2,8192]{2,1,0:T(2,128)(2,1)}, u32[]{:S(2)}, u32[]{:S(2)}) %all-to-all-start) | async-done | bytes 2097184 | tf_op jit(solution)/shard_map/all_to_all | solution.py:66
  128.4 19.1 %all-to-all-start.2 = ((bf16[64,2,8192]{2,1,0:T(2,128)(2,1)}), bf16[64,2,8192]{2,1,0:T(2,128)(2,1)S(1)}, u32[]{:S(2)}, u32[]{:S(2)}) async-start(bf16[64,2,8192]{2,1,0:T(2,128)(2,1)} %reshape.218), calls=%async_computation.2 | async-start | bytes 4194304 | tf_op jit(solution)/shard_map/all_to_all | solution.py:66
  149.1 10.5 %reshape.215 = bf16[64,1,16384]{2,1,0:T(2,128)(2,1)} reshape(bf16[64,2,8192]{2,1,0:T(2,128)(2,1)} %all-to-all-done) | data formatting | bytes 4194304
  159.6 4.5 copy.151
  166.1 2.8 reshape.212
  168.8 73.9 %all-to-all-done.2 = bf16[64,2,8192]{2,1,0:T(2,128)(2,1)S(1)} async-done(((bf16[64,2,8192]{2,1,0:T(2,128)(2,1)}), bf16[64,2,8192]{2,1,0:T(2,128)(2,1)S(1)}, u32[]{:S(2)}, u32[]{:S(2)}) %all-to-all-start.2) | async-done | bytes 2097184 | tf_op jit(solution)/shard_map/all_to_all | solution.py:66
  242.7 6.8 %reshape.219 = bf16[64,1,16384]{2,1,0:T(2,128)(2,1)} reshape(bf16[64,2,8192]{2,1,0:T(2,128)(2,1)S(1)} %all-to-all-done.2) | data formatting | bytes 4194304
  249.5 4.5 copy.150
  257.6 2.9 multiply_convert_fusion.3
  261.1 2.5 fusion.64
  266.0 2.6 copy.75
  275.1 2.9 fusion.14
  285.9 3.1 fusion.11
  290.1 3.0 fusion.13
  297.4 4.1 copy.88
  301.5 2.8 reshape.210
  304.3 3.2 multiply_convert_fusion.2
  307.6 2.6 reduce.4
  311.8 13.2 %all-to-all-start.1 = ((bf16[64,2,4096]{2,1,0:T(2,128)(2,1)}), bf16[64,2,4096]{2,1,0:T(2,128)(2,1)}, u32[]{:S(2)}, u32[]{:S(2)}) async-start(bf16[64,2,4096]{2,1,0:T(2,128)(2,1)} %reshape.216), calls=%async_computation.1 | async-start | bytes 2097152 | tf_op jit(solution)/shard_map/all_to_all | solution.py:76
  327.1 2.7 reshape.220
  329.8 46.2 %all-to-all-done.1 = bf16[64,2,4096]{2,1,0:T(2,128)(2,1)} async-done(((bf16[64,2,4096]{2,1,0:T(2,128)(2,1)}), bf16[64,2,4096]{2,1,0:T(2,128)(2,1)}, u32[]{:S(2)}, u32[]{:S(2)}) %all-to-all-start.1) | async-done | bytes 1048608 | tf_op jit(solution)/shard_map/all_to_all | solution.py:76
  376.0 8.4 %all-to-all-start.3 = ((bf16[64,2,4096]{2,1,0:T(2,128)(2,1)}), bf16[64,2,4096]{2,1,0:T(2,128)(2,1)}, u32[]{:S(2)}, u32[]{:S(2)}) async-start(bf16[64,2,4096]{2,1,0:T(2,128)(2,1)} %reshape.220), calls=%async_computation.3 | async-start | bytes 2097152 | tf_op jit(solution)/shard_map/all_to_all | solution.py:76
  393.7 112.9 %psum.7 = f32[1024]{0:T(1024)} all-reduce(f32[1024]{0:T(1024)S(1)} %add_bitcast_fusion), channel_id=1, replica_groups=mesh['grp'=8,'spec'=64] {'grp','spec'}, use_global_device_ids=true, to_apply=%region_10.11 | all-reduce | flops 1024 | bytes 8192 | tf_op jit(solution)/shard_map/psum | solution.py:85
  506.6 7.5 %reshape.217 = bf16[64,1,8192]{2,1,0:T(2,128)(2,1)} reshape(bf16[64,2,4096]{2,1,0:T(2,128)(2,1)} %all-to-all-done.1) | data formatting | bytes 2097152
  514.1 3.0 fusion.26
  517.2 7.5 %reshape.221 = bf16[64,1,8192]{2,1,0:T(2,128)(2,1)} reshape(bf16[64,2,4096]{2,1,0:T(2,128)(2,1)} %all-to-all-done.3) | data formatting | bytes 2097152
  524.7 3.1 fusion.4
  (101 shorter events, 53.4 us)
Async XLA Ops:
  2.3 3.3 copy-start.27
  2.3 36.9 %copy-start.25 = (pred[64]{0:T(512)(128)(4,1)}, pred[64]{0:T(512)(128)(4,1)S(1)}, u32[]{:S(2)}) copy-start(pred[64]{0:T(512)(128)(4,1)S(1)} %get-tuple-element.12) | copy-start | bytes 196
  4.0 1.7 copy-start.20
  17.2 111.3 %all-to-all-start = ((bf16[64,2,8192]{2,1,0:T(2,128)(2,1)}), bf16[64,2,8192]{2,1,0:T(2,128)(2,1)}, u32[]{:S(2)}, u32[]{:S(2)}) async-start(bf16[64,2,8192]{2,1,0:T(2,128)(2,1)} %reshape.214), calls=%async_computation | async-start | bytes 4194304 | tf_op jit(solution)/shard_map/all_to_all | solution.py:66
  47.8 99.8 %copy-start.15 = (bf16[1,192,1024]{2,1,0:T(8,128)(2,1)S(1)}, bf16[1,192,1024]{2,1,0:T(8,128)(2,1)}, u32[]{:S(2)}) copy-start(bf16[1,192,1024]{2,1,0:T(8,128)(2,1)} %param.8) | copy-start | bytes 1179652
  47.8 99.9 %copy-start.16 = (bf16[1,192,1024]{2,1,0:T(8,128)(2,1)S(1)}, bf16[1,192,1024]{2,1,0:T(8,128)(2,1)}, u32[]{:S(2)}) copy-start(bf16[1,192,1024]{2,1,0:T(8,128)(2,1)} %param.9) | copy-start | bytes 1179652
  47.8 100.7 %copy-start.22 = (f32[1024]{0:T(1024)S(1)}, f32[1024]{0:T(1024)}, u32[]{:S(2)}) copy-start(f32[1024]{0:T(1024)} %param.11) | copy-start | bytes 12292
  128.4 114.3 %all-to-all-start.2 = ((bf16[64,2,8192]{2,1,0:T(2,128)(2,1)}), bf16[64,2,8192]{2,1,0:T(2,128)(2,1)S(1)}, u32[]{:S(2)}, u32[]{:S(2)}) async-start(bf16[64,2,8192]{2,1,0:T(2,128)(2,1)} %reshape.218), calls=%async_computation.2 | async-start | bytes 4194304 | tf_op jit(solution)/shard_map/all_to_all | solution.py:66
  268.6 2.5 copy-start.10
  268.6 2.5 copy-start.17
  271.0 2.5 copy-start.1
  273.5 1.6 copy-start
  275.1 2.9 copy-start.5
  275.1 2.9 copy-start.2
  285.9 3.3 copy-start.12
  285.9 3.5 copy-start.14
  285.9 3.6 copy-start.18
  290.1 3.0 copy-start.8
  290.1 3.0 copy-start.4
  301.5 2.8 copy-start.19
  310.2 14.9 %copy-start.11 = (bf16[64,1,8192]{2,0,1:T(8,128)(2,1)S(1)}, bf16[64,1,8192]{2,0,1:T(8,128)(2,1)}, u32[]{:S(2)}) copy-start(bf16[64,1,8192]{2,0,1:T(8,128)(2,1)} %get-tuple-element.8) | copy-start | bytes 3145732
  311.8 64.2 %all-to-all-start.1 = ((bf16[64,2,4096]{2,1,0:T(2,128)(2,1)}), bf16[64,2,4096]{2,1,0:T(2,128)(2,1)}, u32[]{:S(2)}, u32[]{:S(2)}) async-start(bf16[64,2,4096]{2,1,0:T(2,128)(2,1)} %reshape.216), calls=%async_computation.1 | async-start | bytes 2097152 | tf_op jit(solution)/shard_map/all_to_all | solution.py:76
  327.1 57.3 %copy-start.7 = (bf16[8,512,192]{1,2,0:T(8,128)(2,1)S(1)}, bf16[8,512,192]{1,2,0:T(8,128)(2,1)}, u32[]{:S(2)}) copy-start(bf16[8,512,192]{1,2,0:T(8,128)(2,1)} %copy-done.6) | copy-start | bytes 4718596
  376.0 141.2 %all-to-all-start.3 = ((bf16[64,2,4096]{2,1,0:T(2,128)(2,1)}), bf16[64,2,4096]{2,1,0:T(2,128)(2,1)}, u32[]{:S(2)}, u32[]{:S(2)}) async-start(bf16[64,2,4096]{2,1,0:T(2,128)(2,1)} %reshape.220), calls=%async_computation.3 | async-start | bytes 2097152 | tf_op jit(solution)/shard_map/all_to_all | solution.py:76
  384.4 2.2 copy-start.13
  388.8 3.0 copy-start.3
  389.7 2.1 copy-start.9
  391.8 1.9 copy-start.23
  391.9 1.9 copy-start.24
  392.8 121.4 %copy-start.21 = (s32[64,1]{0,1:T(1,128)S(1)}, s32[64,1]{0,1:T(1,128)}, u32[]{:S(2)}) copy-start(s32[64,1]{0,1:T(1,128)} %param.10) | copy-start | bytes 772
  392.8 121.3 %copy-start.28 = (pred[64]{0:T(512)(128)(4,1)S(1)}, pred[64]{0:T(512)(128)(4,1)}, u32[]{:S(2)}) copy-start(pred[64]{0:T(512)(128)(4,1)} %copy-done.27) | copy-start | bytes 196
  517.2 7.5 %copy-start.26 = (pred[64]{0:T(512)(128)(4,1)S(1)}, pred[64]{0:T(512)(128)(4,1)}, u32[]{:S(2)}) copy-start(pred[64]{0:T(512)(128)(4,1)} %copy-done.25) | copy-start | bytes 196
  (1 other events, 1.1 us)

commit v2 on v1

v2 whole, which is shorter than its diff:
```python
import math

import jax
import jax.numpy as jnp
from jax import lax
from jax.sharding import PartitionSpec as P

HEADS = 8
HEAD_DIM = 128
CAP = 2
PIECES = 3


def attend_backward(recv_rows, recv_grads, keys_here, values_here, query_gain):
    total_rows, width = recv_rows.shape
    head_dim = width // HEADS
    inv_root = 1.0 / math.sqrt(HEAD_DIM)
    gained = (recv_rows.astype(jnp.float32) * query_gain).astype(jnp.bfloat16)
    key_count = keys_here.shape[0]
    q_heads = gained.reshape(total_rows, HEADS, head_dim)
    g_heads = recv_grads.reshape(total_rows, HEADS, head_dim)
    k_heads = keys_here.reshape(key_count, HEADS, head_dim)
    v_heads = values_here.reshape(key_count, HEADS, head_dim)
    f32 = jnp.float32
    scores = jnp.einsum("rhd,khd->hrk", q_heads, k_heads, preferred_element_type=f32) * inv_root
    top = jnp.max(scores, axis=2, keepdims=True)
    expo = jnp.exp(scores - top)
    probs = expo / jnp.sum(expo, axis=2, keepdims=True)
    probs_b = probs.astype(jnp.bfloat16)
    attended = jnp.einsum("hrk,khd->rhd", probs_b, v_heads, preferred_element_type=f32)
    delta = jnp.sum(g_heads.astype(f32) * attended, axis=2)
    dprobs = jnp.einsum("rhd,khd->hrk", g_heads, v_heads, preferred_element_type=f32)
    dscores = (probs * (dprobs - delta.T[:, :, None])).astype(jnp.bfloat16)
    q_grad = jnp.einsum("hrk,khd->rhd", dscores, k_heads, preferred_element_type=f32) * inv_root
    k_grad = jnp.einsum("hrk,rhd->khd", dscores, q_heads, preferred_element_type=f32) * inv_root
    v_grad = jnp.einsum("hrk,rhd->khd", probs_b, g_heads, preferred_element_type=f32)
    gained_grad = q_grad.reshape(total_rows, width)
    return (gained_grad, k_grad.reshape(key_count, width), v_grad.reshape(key_count, width))


def split_pieces(value, count):
    pieces = []
    rest = value
    for _ in range(count - 1):
        head = lax.reduce_precision(rest, exponent_bits=8, mantissa_bits=7)
        pieces.append(head)
        rest = rest - head
    pieces.append(rest)
    return jnp.stack(pieces).astype(jnp.bfloat16)


def shards(queries, out_grad, spec_keys, spec_values, owner_of, query_gain):
    peers = lax.axis_size("spec")
    cand_count = owner_of.shape[0]
    width = queries.shape[1]
    qtok_here = queries.shape[0] // cand_count
    slot_count = peers * CAP
    target = owner_of[:, 0]
    onehot = (target[:, None] == jnp.arange(peers, dtype=jnp.int32)[None, :]).astype(jnp.int32)
    earlier = jnp.cumsum(onehot, axis=0) - onehot
    position = jnp.sum(earlier * onehot, axis=1)
    slot_index = target * CAP + position
    placing = (jnp.arange(slot_count, dtype=jnp.int32)[:, None] == slot_index[None, :]).astype(
        jnp.bfloat16
    )
    flat_both = jnp.concatenate(
        [queries.reshape(cand_count, qtok_here * width), out_grad.reshape(cand_count, qtok_here * width)],
        axis=1,
    )
    send_both = jnp.dot(placing, flat_both, preferred_element_type=jnp.float32).astype(jnp.bfloat16)
    send_both = send_both.reshape(peers, CAP * 2 * qtok_here, width)
    recv_both = lax.all_to_all(send_both, "spec", split_axis=0, concat_axis=0, tiled=True)
    recv_both = recv_both.reshape(slot_count, 2, qtok_here, width)
    recv_rows = recv_both[:, 0].reshape(slot_count * qtok_here, width)
    recv_cotan = recv_both[:, 1].reshape(slot_count * qtok_here, width)
    gained_grad, key_grad, value_grad = attend_backward(
        recv_rows, recv_cotan, spec_keys[0], spec_values[0], query_gain
    )
    partial_value = jnp.sum(recv_rows.astype(jnp.float32) * gained_grad, axis=0)
    going_back = (gained_grad * query_gain).astype(jnp.bfloat16).reshape(
        peers, CAP * qtok_here, width
    )
    gain_rows = jnp.broadcast_to(split_pieces(partial_value, PIECES)[None], (peers, PIECES, width))
    going_back = jnp.concatenate([going_back, gain_rows], axis=1)
    came_back = lax.all_to_all(going_back, "spec", split_axis=0, concat_axis=0, tiled=True)
    spec_sum = jnp.sum(came_back[:, CAP * qtok_here :].astype(jnp.float32), axis=(0, 1))
    gain_grad = lax.psum(spec_sum, "grp")
    came_back = came_back[:, : CAP * qtok_here]
    home_grads = jnp.dot(
        placing.T, came_back.reshape(slot_count, qtok_here * width), preferred_element_type=jnp.float32
    ).astype(jnp.bfloat16)
    query_grad = home_grads.reshape(cand_count * qtok_here, width)
    return (
        query_grad,
        key_grad.astype(jnp.bfloat16)[None],
        value_grad.astype(jnp.bfloat16)[None],
        gain_grad,
    )


def solution(mesh):
    return jax.shard_map(
        shards,
        mesh=mesh,
        in_specs=(
            P(("grp", "spec"), None),
            P(("grp", "spec"), None),
            P(("grp", "spec"), None, None),
            P(("grp", "spec"), None, None),
            P(("grp", "spec"), None),
            P(),
        ),
        out_specs=(
            P(("grp", "spec"), None),
            P(("grp", "spec"), None, None),
            P(("grp", "spec"), None, None),
            P(),
        ),
        check_vma=False,
    )
```

time: 537 us -> 455 us (0.85); the launches traced: 529 us -> 454 us
  waiting for transfers between devices: 201 us -> 316 us
  blocking collectives: 113 us -> 21.6 us
  local copies, waits for them, and re-layouts: 90.9 us -> 39.9 us
  starting transfers between devices: 62.8 us -> 37.5 us
  other arithmetic: 32.1 us -> 19.2 us
  matrix products: 28.5 us -> 18.9 us
    psum x1, blocking collectives: 113 us -> 21.6 us  [shards(): gain_grad = lax.psum(spec_sum, 'grp')]
    all_to_all x2 -> x1, waiting for transfers between devices: 46.2 us -> 132 us  [shards(): lax.all_to_all(going_back, 'spec', split_axis=0, concat_axis=0, tiled=True)]
    unnamed x73 -> x20, local copies, waits for them, and re-layouts: 58.2 us -> 6.47 us
    all_to_all x2 -> x1, waiting for transfers between devices: 155 us -> 184 us  [shards(): lax.all_to_all(send_both, 'spec', split_axis=0, concat_axis=0, tiled=True)]
    all_to_all x2 -> x1, starting transfers between devices: 41.1 us -> 22.3 us  [shards(): lax.all_to_all(send_both, 'spec', split_axis=0, concat_axis=0, tiled=True)]
    reshape x1 -> x3, local copies, waits for them, and re-layouts: 1.3 us -> 13.9 us  [the longest x1 7.41 us: shards(): send_both = send_both.reshape(peers, CAP * 2 * qtok_here, width)]
    all_to_all x2 -> x0, other arithmetic: 8.3 us -> none  [shards(): lax.all_to_all(send_both, 'spec', split_axis=0, concat_axis=0, tiled=True)]
    another operation x4 -> x1, local copies, waits for them, and re-layouts: 9.7 us -> 3.05 us  [attend_backward(): g_heads = recv_grads.reshape(total_rows, HEADS, head_dim)]
  transfers between devices with their start and end apart: 4 -> 2, of which waited for: 3 -> 2; matrix products, arithmetic and copies ran while one was open for 10% -> 2% of each run, Pallas kernels for 0% -> 0%
where the time goes in v2:
time: 455 us; the launch traced here: 454 us
  waiting for transfers between devices  316 us (69%)
  local copies, waits for them, and re-layouts  39.9 us (9%)
  starting transfers between devices  37.5 us (8%)
  blocking collectives  21.6 us (5%)
  other arithmetic  19.2 us (4%)
  matrix products  18.9 us (4%)
    all_to_all x1, waiting for transfers between devices, shards(): lax.all_to_all(send_both, 'spec', split_axis=0, concat_axis=0, tiled=True)  184 us
    all_to_all x1, waiting for transfers between devices, shards(): lax.all_to_all(going_back, 'spec', split_axis=0, concat_axis=0, tiled=True)  132 us
    all_to_all x1, starting transfers between devices, shards(): lax.all_to_all(send_both, 'spec', split_axis=0, concat_axis=0, tiled=True)  22.3 us
    psum x1, blocking collectives, shards(): gain_grad = lax.psum(spec_sum, 'grp')  21.6 us
    all_to_all x1, starting transfers between devices, shards(): lax.all_to_all(going_back, 'spec', split_axis=0, concat_axis=0, tiled=True)  15.2 us
  transfers between devices with their start and end apart: 2, of which 2 were waited for; matrix products, arithmetic and copies ran while one was open for 2% of the time, Pallas kernels for 0%

profile of v2, /device:TPU:1, one launch (start us, length us, event | category | flops | bytes accessed | tf_op | source)
XLA Modules:
  0.0 454.1 jit_solution(17783786363941652475)
XLA Ops:
  3.0 1.6 reshape.147
  4.5 1.6 reshape.148
  6.1 3.2 convolution_convert_fusion
  9.3 7.4 %reshape.149 = bf16[64,32,1024]{2,1,0:T(8,128)(2,1)} reshape(bf16[128,16384]{1,0:T(8,128)(2,1)} %convolution_convert_fusion) | data formatting | bytes 8388608 | tf_op jit(solution)/shard_map/reshape | solution.py:71
  16.7 22.3 %all-to-all-start = ((bf16[64,32,1024]{2,1,0:T(8,128)(2,1)}), bf16[64,32,1024]{2,1,0:T(8,128)(2,1)}, u32[]{:S(2)}, u32[]{:S(2)}) async-start(bf16[64,32,1024]{2,1,0:T(8,128)(2,1)} %reshape.149), calls=%async_computation | async-start | bytes 8388608 | tf_op jit(solution)/shard_map/all_to_all | solution.py:72
  39.2 184.3 %all-to-all-done = bf16[64,32,1024]{2,1,0:T(8,128)(2,1)} async-done(((bf16[64,32,1024]{2,1,0:T(8,128)(2,1)}), bf16[64,32,1024]{2,1,0:T(8,128)(2,1)}, u32[]{:S(2)}, u32[]{:S(2)}) %all-to-all-start) | async-done | bytes 4194336 | tf_op jit(solution)/shard_map/all_to_all | solution.py:72
  223.5 3.1 convert_bitcast_fusion
  226.5 2.9 copy.41
  230.1 3.1 copy.32
  233.1 2.4 multiply_convert_fusion.2
  235.6 1.3 copy-done.1
  236.9 1.0 fusion.13
  237.9 5.1 %fusion.35 = (f32[8,1024]{1,0:T(8,128)S(1)}, f32[8,1024,192]{1,2,0:T(8,128)S(1)}) fusion(f32[8,1024,192]{1,2,0:T(8,128)S(1)} %fusion.13), kind=kOutput, calls=%fused_computation.52 | output fusion | flops 6291647 | bytes 12615680 | tf_op jit(solution)/shard_map/sub | solution.py:27
  243.0 1.0 fusion.7
  244.6 1.2 fusion.4
  245.8 1.3 multiply_convert_fusion
  248.0 1.9 fusion.5
  249.9 4.4 copy.35
  254.3 4.9 %reshape.151 = f32[64,16,1024]{2,1,0:T(8,128)} reshape(f32[1024,8,128]{2,1,0:T(8,128)} %copy.35) | data formatting | bytes 8388608 | tf_op jit(solution)/shard_map/reshape | solution.py:37
  259.2 2.8 multiply_convert_fusion.1
  262.1 2.2 pad_maximum_fusion
  264.4 15.2 %all-to-all-start.1 = ((bf16[64,19,1024]{2,1,0:T(8,128)(2,1)}), bf16[64,19,1024]{2,1,0:T(8,128)(2,1)S(1)}, u32[]{:S(2)}, u32[]{:S(2)}) async-start(bf16[64,19,1024]{2,1,0:T(8,128)(2,1)} %pad_maximum_fusion), calls=%async_computation.1 | async-start | bytes 6291456 | tf_op jit(solution)/shard_map/all_to_all | solution.py:85
  279.6 3.5 fusion.24
  283.4 0.9 convert_element_type.91
  284.3 3.7 fusion.21
  288.3 0.9 convert_element_type.88
  289.2 131.9 %all-to-all-done.1 = bf16[64,19,1024]{2,1,0:T(8,128)(2,1)S(1)} async-done(((bf16[64,19,1024]{2,1,0:T(8,128)(2,1)}), bf16[64,19,1024]{2,1,0:T(8,128)(2,1)S(1)}, u32[]{:S(2)}, u32[]{:S(2)}) %all-to-all-start.1) | async-done | bytes 2490400 | tf_op jit(solution)/shard_map/all_to_all | solution.py:85
  421.1 1.5 slice.18
  422.6 4.2 reshape.152
  426.8 3.1 convolution_convert_fusion.1
  429.9 2.3 reshape.153
  432.5 21.6 %psum.7 = f32[1024]{0:T(1024)} all-reduce(f32[1024]{0:T(1024)S(1)} %convert_reduce_fusion), channel_id=1, replica_groups=mesh['grp'=8,'spec'=64] {'grp'}, use_global_device_ids=true, to_apply=%region_7.8 | all-reduce | flops 1024 | bytes 8192 | tf_op jit(solution)/shard_map/psum | solution.py:87
  (28 shorter events, 5.5 us)
Async XLA Ops:
  16.7 22.3 %copy-start.5 = (bf16[1,192,1024]{2,1,0:T(8,128)(2,1)S(1)}, bf16[1,192,1024]{2,1,0:T(8,128)(2,1)}, u32[]{:S(2)}) copy-start(bf16[1,192,1024]{2,1,0:T(8,128)(2,1)} %param.8) | copy-start | bytes 1179652
  16.7 22.4 %copy-start.6 = (bf16[1,192,1024]{2,1,0:T(8,128)(2,1)S(1)}, bf16[1,192,1024]{2,1,0:T(8,128)(2,1)}, u32[]{:S(2)}) copy-start(bf16[1,192,1024]{2,1,0:T(8,128)(2,1)} %param.9) | copy-start | bytes 1179652
  16.7 206.8 %all-to-all-start = ((bf16[64,32,1024]{2,1,0:T(8,128)(2,1)}), bf16[64,32,1024]{2,1,0:T(8,128)(2,1)}, u32[]{:S(2)}, u32[]{:S(2)}) async-start(bf16[64,32,1024]{2,1,0:T(8,128)(2,1)} %reshape.149), calls=%async_computation | async-start | bytes 8388608 | tf_op jit(solution)/shard_map/all_to_all | solution.py:72
  230.1 3.1 copy-start.7
  235.5 1.3 copy-start.1
  243.0 1.6 copy-start.4
  244.0 1.8 copy-start.3
  245.8 2.2 copy-start
  247.1 2.8 copy-start.2
  264.4 156.7 %all-to-all-start.1 = ((bf16[64,19,1024]{2,1,0:T(8,128)(2,1)}), bf16[64,19,1024]{2,1,0:T(8,128)(2,1)S(1)}, u32[]{:S(2)}, u32[]{:S(2)}) async-start(bf16[64,19,1024]{2,1,0:T(8,128)(2,1)} %pad_maximum_fusion), calls=%async_computation.1 | async-start | bytes 6291456 | tf_op jit(solution)/shard_map/all_to_all | solution.py:85

commit v3 on v2

--- a/solution.py
+++ b/solution.py
@@ -8,7 +8,7 @@
 HEADS = 8
 HEAD_DIM = 128
 CAP = 2
-PIECES = 3
+PIECES = 2
 
 
 def attend_backward(recv_rows, recv_grads, keys_here, values_here, query_gain):
@@ -60,14 +60,14 @@
     earlier = jnp.cumsum(onehot, axis=0) - onehot
     position = jnp.sum(earlier * onehot, axis=1)
     slot_index = target * CAP + position
-    placing = (jnp.arange(slot_count, dtype=jnp.int32)[:, None] == slot_index[None, :]).astype(
-        jnp.bfloat16
-    )
-    flat_both = jnp.concatenate(
-        [queries.reshape(cand_count, qtok_here * width), out_grad.reshape(cand_count, qtok_here * width)],
+    matches = jnp.arange(slot_count, dtype=jnp.int32)[:, None] == slot_index[None, :]
+    source = jnp.argmax(matches, axis=1).astype(jnp.int32)
+    used = jnp.any(matches, axis=1)
+    both = jnp.concatenate(
+        [queries.reshape(cand_count, qtok_here, width), out_grad.reshape(cand_count, qtok_here, width)],
         axis=1,
     )
-    send_both = jnp.dot(placing, flat_both, preferred_element_type=jnp.float32).astype(jnp.bfloat16)
+    send_both = jnp.where(used[:, None, None], jnp.take(both, source, axis=0), jnp.zeros((), both.dtype))
     send_both = send_both.reshape(peers, CAP * 2 * qtok_here, width)
     recv_both = lax.all_to_all(send_both, "spec", split_axis=0, concat_axis=0, tiled=True)
     recv_both = recv_both.reshape(slot_count, 2, qtok_here, width)
@@ -86,9 +86,7 @@
     spec_sum = jnp.sum(came_back[:, CAP * qtok_here :].astype(jnp.float32), axis=(0, 1))
     gain_grad = lax.psum(spec_sum, "grp")
     came_back = came_back[:, : CAP * qtok_here]
-    home_grads = jnp.dot(
-        placing.T, came_back.reshape(slot_count, qtok_here * width), preferred_element_type=jnp.float32
-    ).astype(jnp.bfloat16)
+    home_grads = jnp.take(came_back.reshape(slot_count, qtok_here, width), slot_index, axis=0)
     query_grad = home_grads.reshape(cand_count * qtok_here, width)
     return (
         query_grad,

time: 455 us -> 445 us (0.978)
  local copies, waits for them, and re-layouts: 39.9 us -> 28.7 us
  other arithmetic: 19.2 us -> 26.7 us
  matrix products: 18.9 us -> 12.7 us
    reshape x5 -> x0, local copies, waits for them, and re-layouts: 17 us -> none  [the longest x1 7.41 us: shards(): send_both = send_both.reshape(peers, CAP * 2 * qtok_here, width)]
    dot_general x2 -> x0, matrix products: 6.27 us -> none  [the longest x1 3.2 us: shards(): jnp.dot(placing, flat_both, preferred_element_type=jnp.float32)]
    select_n x0 -> x3, other arithmetic: none -> 5.02 us  [the longest x1 3.88 us: shards(): jnp.where(used[:, None, None], jnp.take(both, source, axis=0), jnp.zeros(...]
    gather x0 -> x2, local copies, waits for them, and re-layouts: none -> 4.99 us  [the longest x1 2.79 us: shards(): jnp.take(both, source, axis=0)]
where the time goes in v3:
time: 445 us; the launch traced here: 444 us
  waiting for transfers between devices  315 us (71%)
  starting transfers between devices  37.2 us (8%)
  local copies, waits for them, and re-layouts  28.7 us (6%)
  other arithmetic  26.7 us (6%)
  blocking collectives  22.8 us (5%)
  matrix products  12.7 us (3%)
    all_to_all x1, waiting for transfers between devices, shards(): lax.all_to_all(send_both, 'spec', split_axis=0, concat_axis=0, tiled=True)  184 us
    all_to_all x1, waiting for transfers between devices, shards(): lax.all_to_all(going_back, 'spec', split_axis=0, concat_axis=0, tiled=True)  131 us
    psum x1, blocking collectives, shards(): gain_grad = lax.psum(spec_sum, 'grp')  22.8 us
    all_to_all x1, starting transfers between devices, shards(): lax.all_to_all(send_both, 'spec', split_axis=0, concat_axis=0, tiled=True)  22.3 us
    all_to_all x1, starting transfers between devices, shards(): lax.all_to_all(going_back, 'spec', split_axis=0, concat_axis=0, tiled=True)  14.8 us
  transfers between devices with their start and end apart: 2, of which 2 were waited for; matrix products, arithmetic and copies ran while one was open for 2% of the time, Pallas kernels for 0%

profile of v3, /device:TPU:1, one launch (start us, length us, event | category | flops | bytes accessed | tf_op | source)
XLA Modules:
  0.0 444.1 jit_solution(4465424294843375575)
XLA Ops:
  1.5 0.8 select_reduce_fusion
  4.4 1.8 pad_maximum_fusion.1
  6.2 2.8 gather_fusion
  9.0 3.9 fusion.5
  12.9 22.3 %all-to-all-start = ((bf16[64,32,1024]{2,1,0:T(8,128)(2,1)}), bf16[64,32,1024]{2,1,0:T(8,128)(2,1)}, u32[]{:S(2)}, u32[]{:S(2)}) async-start(bf16[64,32,1024]{2,1,0:T(8,128)(2,1)} %fusion.5), calls=%async_computation | async-start | bytes 8388608 | tf_op jit(solution)/shard_map/all_to_all | solution.py:72
  35.4 184.3 %all-to-all-done = bf16[64,32,1024]{2,1,0:T(8,128)(2,1)} async-done(((bf16[64,32,1024]{2,1,0:T(8,128)(2,1)}), bf16[64,32,1024]{2,1,0:T(8,128)(2,1)}, u32[]{:S(2)}, u32[]{:S(2)}) %all-to-all-start) | async-done | bytes 4194336 | tf_op jit(solution)/shard_map/all_to_all | solution.py:72
  219.7 3.1 convert_bitcast_fusion
  222.8 2.9 copy.66
  226.3 3.1 copy.57
  229.4 2.4 multiply_convert_fusion.2
  231.8 1.3 copy-done.1
  233.1 1.0 fusion.11
  234.1 5.1 %fusion.31 = (f32[8,1024]{1,0:T(8,128)S(1)}, f32[8,1024,192]{1,2,0:T(8,128)S(1)}) fusion(f32[8,1024,192]{1,2,0:T(8,128)S(1)} %fusion.11), kind=kOutput, calls=%fused_computation.57 | output fusion | flops 6291647 | bytes 12615680 | tf_op jit(solution)/shard_map/sub | solution.py:27
  239.2 1.0 fusion.8
  240.8 1.2 fusion.4
  242.0 1.3 multiply_convert_fusion
  243.3 0.9 copy-done
  244.2 1.9 fusion.6
  246.1 4.4 copy.60
  250.5 4.9 %reshape.146 = f32[64,16,1024]{2,1,0:T(8,128)} reshape(f32[1024,8,128]{2,1,0:T(8,128)} %copy.60) | data formatting | bytes 8388608 | tf_op jit(solution)/shard_map/reshape | solution.py:37
  255.4 2.8 multiply_convert_fusion.1
  258.4 2.2 pad_maximum_fusion
  260.6 14.8 %all-to-all-start.1 = ((bf16[64,18,1024]{2,1,0:T(8,128)(2,1)}), bf16[64,18,1024]{2,1,0:T(8,128)(2,1)S(1)}, u32[]{:S(2)}, u32[]{:S(2)}) async-start(bf16[64,18,1024]{2,1,0:T(8,128)(2,1)} %pad_maximum_fusion), calls=%async_computation.1 | async-start | bytes 6291456 | tf_op jit(solution)/shard_map/all_to_all | solution.py:85
  275.7 3.5 fusion.22
  279.5 0.9 convert_element_type.82
  280.4 3.7 fusion.19
  284.4 0.9 convert_element_type.79
  285.3 130.8 %all-to-all-done.1 = bf16[64,18,1024]{2,1,0:T(8,128)(2,1)S(1)} async-done(((bf16[64,18,1024]{2,1,0:T(8,128)(2,1)}), bf16[64,18,1024]{2,1,0:T(8,128)(2,1)S(1)}, u32[]{:S(2)}, u32[]{:S(2)}) %all-to-all-start.1) | async-done | bytes 2359328 | tf_op jit(solution)/shard_map/all_to_all | solution.py:85
  416.4 22.8 %psum.7 = f32[1024]{0:T(1024)} all-reduce(f32[1024]{0:T(1024)S(1)} %convert_reduce_fusion), channel_id=1, replica_groups=mesh['grp'=8,'spec'=64] {'grp'}, use_global_device_ids=true, to_apply=%region_9.10 | all-reduce | flops 1024 | bytes 8192 | tf_op jit(solution)/shard_map/psum | solution.py:87
  439.1 1.6 slice.22
  440.7 2.2 gather_fusion.1
  442.9 1.1 bitcast_select_fusion.1
  (45 shorter events, 5.4 us)
Async XLA Ops:
  12.9 22.3 %copy-start.5 = (bf16[1,192,1024]{2,1,0:T(8,128)(2,1)S(1)}, bf16[1,192,1024]{2,1,0:T(8,128)(2,1)}, u32[]{:S(2)}) copy-start(bf16[1,192,1024]{2,1,0:T(8,128)(2,1)} %param.8) | copy-start | bytes 1179652
  12.9 22.4 %copy-start.6 = (bf16[1,192,1024]{2,1,0:T(8,128)(2,1)S(1)}, bf16[1,192,1024]{2,1,0:T(8,128)(2,1)}, u32[]{:S(2)}) copy-start(bf16[1,192,1024]{2,1,0:T(8,128)(2,1)} %param.9) | copy-start | bytes 1179652
  12.9 206.8 %all-to-all-start = ((bf16[64,32,1024]{2,1,0:T(8,128)(2,1)}), bf16[64,32,1024]{2,1,0:T(8,128)(2,1)}, u32[]{:S(2)}, u32[]{:S(2)}) async-start(bf16[64,32,1024]{2,1,0:T(8,128)(2,1)} %fusion.5), calls=%async_computation | async-start | bytes 8388608 | tf_op jit(solution)/shard_map/all_to_all | solution.py:72
  225.7 3.7 copy-start.7
  231.8 1.3 copy-start.1
  239.2 1.6 copy-start.4
  240.2 1.8 copy-start.3
  242.0 2.2 copy-start
  243.3 2.8 copy-start.2
  260.6 14.9 %copy-start.8 = (s32[64,1]{0,1:T(1,128)S(1)}, s32[64,1]{0,1:T(1,128)}, u32[]{:S(2)}) copy-start(s32[64,1]{0,1:T(1,128)} %param.10) | copy-start | bytes 772
  260.6 155.6 %all-to-all-start.1 = ((bf16[64,18,1024]{2,1,0:T(8,128)(2,1)}), bf16[64,18,1024]{2,1,0:T(8,128)(2,1)S(1)}, u32[]{:S(2)}, u32[]{:S(2)}) async-start(bf16[64,18,1024]{2,1,0:T(8,128)(2,1)} %pad_maximum_fusion), calls=%async_computation.1 | async-start | bytes 6291456 | tf_op jit(solution)/shard_map/all_to_all | solution.py:85

commit v4 on v3

--- a/solution.py
+++ b/solution.py
@@ -14,28 +14,32 @@
 def attend_backward(recv_rows, recv_grads, keys_here, values_here, query_gain):
     total_rows, width = recv_rows.shape
     head_dim = width // HEADS
+    key_count = keys_here.shape[0]
     inv_root = 1.0 / math.sqrt(HEAD_DIM)
-    gained = (recv_rows.astype(jnp.float32) * query_gain).astype(jnp.bfloat16)
-    key_count = keys_here.shape[0]
-    q_heads = gained.reshape(total_rows, HEADS, head_dim)
-    g_heads = recv_grads.reshape(total_rows, HEADS, head_dim)
-    k_heads = keys_here.reshape(key_count, HEADS, head_dim)
-    v_heads = values_here.reshape(key_count, HEADS, head_dim)
     f32 = jnp.float32
-    scores = jnp.einsum("rhd,khd->hrk", q_heads, k_heads, preferred_element_type=f32) * inv_root
+    gain_hm = query_gain.reshape(HEADS, 1, head_dim)
+    raw_hm = recv_rows.reshape(total_rows, HEADS, head_dim).transpose(1, 0, 2)
+    g_hm = recv_grads.reshape(total_rows, HEADS, head_dim).transpose(1, 0, 2)
+    k_hm = keys_here.reshape(key_count, HEADS, head_dim).transpose(1, 0, 2)
+    v_hm = values_here.reshape(key_count, HEADS, head_dim).transpose(1, 0, 2)
+    gained_hm = (raw_hm.astype(f32) * gain_hm).astype(jnp.bfloat16)
+    scores = jnp.einsum("hrd,hkd->hrk", gained_hm, k_hm, preferred_element_type=f32) * inv_root
     top = jnp.max(scores, axis=2, keepdims=True)
     expo = jnp.exp(scores - top)
     probs = expo / jnp.sum(expo, axis=2, keepdims=True)
     probs_b = probs.astype(jnp.bfloat16)
-    attended = jnp.einsum("hrk,khd->rhd", probs_b, v_heads, preferred_element_type=f32)
-    delta = jnp.sum(g_heads.astype(f32) * attended, axis=2)
-    dprobs = jnp.einsum("rhd,khd->hrk", g_heads, v_heads, preferred_element_type=f32)
-    dscores = (probs * (dprobs - delta.T[:, :, None])).astype(jnp.bfloat16)
-    q_grad = jnp.einsum("hrk,khd->rhd", dscores, k_heads, preferred_element_type=f32) * inv_root
-    k_grad = jnp.einsum("hrk,rhd->khd", dscores, q_heads, preferred_element_type=f32) * inv_root
-    v_grad = jnp.einsum("hrk,rhd->khd", probs_b, g_heads, preferred_element_type=f32)
-    gained_grad = q_grad.reshape(total_rows, width)
-    return (gained_grad, k_grad.reshape(key_count, width), v_grad.reshape(key_count, width))
+    attended = jnp.einsum("hrk,hkd->hrd", probs_b, v_hm, preferred_element_type=f32)
+    delta = jnp.sum(g_hm.astype(f32) * attended, axis=2, keepdims=True)
+    dprobs = jnp.einsum("hrd,hkd->hrk", g_hm, v_hm, preferred_element_type=f32)
+    dscores = (probs * (dprobs - delta)).astype(jnp.bfloat16)
+    q_grad = jnp.einsum("hrk,hkd->hrd", dscores, k_hm, preferred_element_type=f32) * inv_root
+    k_grad = jnp.einsum("hrk,hrd->hkd", dscores, gained_hm, preferred_element_type=f32) * inv_root
+    v_grad = jnp.einsum("hrk,hrd->hkd", probs_b, g_hm, preferred_element_type=f32)
+    gain_part = jnp.sum(raw_hm.astype(f32) * q_grad, axis=1).reshape(width)
+    going_back = (q_grad * gain_hm).astype(jnp.bfloat16).transpose(1, 0, 2).reshape(total_rows, width)
+    key_grad = k_grad.astype(jnp.bfloat16).transpose(1, 0, 2).reshape(key_count, width)
+    value_grad = v_grad.astype(jnp.bfloat16).transpose(1, 0, 2).reshape(key_count, width)
+    return (going_back, gain_part, key_grad, value_grad)
 
 
 def split_pieces(value, count):
@@ -67,19 +71,17 @@
         [queries.reshape(cand_count, qtok_here, width), out_grad.reshape(cand_count, qtok_here, width)],
         axis=1,
     )
-    send_both = jnp.where(used[:, None, None], jnp.take(both, source, axis=0), jnp.zeros((), both.dtype))
+    source = jnp.where(used, source, cand_count)
+    send_both = jnp.take(both, source, axis=0, mode="fill", fill_value=0)
     send_both = send_both.reshape(peers, CAP * 2 * qtok_here, width)
     recv_both = lax.all_to_all(send_both, "spec", split_axis=0, concat_axis=0, tiled=True)
     recv_both = recv_both.reshape(slot_count, 2, qtok_here, width)
     recv_rows = recv_both[:, 0].reshape(slot_count * qtok_here, width)
     recv_cotan = recv_both[:, 1].reshape(slot_count * qtok_here, width)
-    gained_grad, key_grad, value_grad = attend_backward(
+    going_back, partial_value, key_grad, value_grad = attend_backward(
         recv_rows, recv_cotan, spec_keys[0], spec_values[0], query_gain
     )
-    partial_value = jnp.sum(recv_rows.astype(jnp.float32) * gained_grad, axis=0)
-    going_back = (gained_grad * query_gain).astype(jnp.bfloat16).reshape(
-        peers, CAP * qtok_here, width
-    )
+    going_back = going_back.reshape(peers, CAP * qtok_here, width)
     gain_rows = jnp.broadcast_to(split_pieces(partial_value, PIECES)[None], (peers, PIECES, width))
     going_back = jnp.concatenate([going_back, gain_rows], axis=1)
     came_back = lax.all_to_all(going_back, "spec", split_axis=0, concat_axis=0, tiled=True)
@@ -90,8 +92,8 @@
     query_grad = home_grads.reshape(cand_count * qtok_here, width)
     return (
         query_grad,
-        key_grad.astype(jnp.bfloat16)[None],
-        value_grad.astype(jnp.bfloat16)[None],
+        key_grad[None],
+        value_grad[None],
         gain_grad,
     )
 

time: 445 us -> 433 us (0.973)
  local copies, waits for them, and re-layouts: 28.7 us -> 16.9 us
    convert_element_type x2 -> x0, other arithmetic: 5.18 us -> none  [the longest x1 2.77 us: shards(): (gained_grad * query_gain).astype(jnp.bfloat16)]
    reshape x1 -> x0, local copies, waits for them, and re-layouts: 4.91 us -> none  [attend_backward(): gained_grad = q_grad.reshape(total_rows, width)]
    unnamed x22 -> x20, local copies, waits for them, and re-layouts: 6.46 us -> 1.79 us
where the time goes in v4:
time: 433 us; the launch traced here: 432 us
  waiting for transfers between devices  313 us (72%)
  starting transfers between devices  38.7 us (9%)
  other arithmetic  24.2 us (6%)
  blocking collectives  22.8 us (5%)
  local copies, waits for them, and re-layouts  16.9 us (4%)
  matrix products  15.4 us (4%)
    all_to_all x1, waiting for transfers between devices, shards(): lax.all_to_all(send_both, 'spec', split_axis=0, concat_axis=0, tiled=True)  183 us
    all_to_all x1, waiting for transfers between devices, shards(): lax.all_to_all(going_back, 'spec', split_axis=0, concat_axis=0, tiled=True)  130 us
    psum x1, blocking collectives, shards(): gain_grad = lax.psum(spec_sum, 'grp')  22.8 us
    all_to_all x1, starting transfers between devices, shards(): lax.all_to_all(send_both, 'spec', split_axis=0, concat_axis=0, tiled=True)  22.1 us
    all_to_all x1, starting transfers between devices, shards(): lax.all_to_all(going_back, 'spec', split_axis=0, concat_axis=0, tiled=True)  16.5 us
  transfers between devices with their start and end apart: 2, of which 2 were waited for; matrix products, arithmetic and copies ran while one was open for 2% of the time, Pallas kernels for 0%

profile of v4, /device:TPU:1, one launch (start us, length us, event | category | flops | bytes accessed | tf_op | source)
XLA Modules:
  0.0 432.1 jit_solution(15981250231091073433)
XLA Ops:
  0.6 0.7 fusion.35
  1.5 0.8 select_reduce_fusion
  2.3 0.7 multiply_add_fusion
  3.0 0.6 iota_reduce_fusion
  4.1 1.8 pad_maximum_fusion.1
  5.9 2.8 gather_fusion
  8.6 3.7 bitcast_select_fusion
  12.4 22.1 %all-to-all-start = ((bf16[64,32,1024]{2,1,0:T(8,128)(2,1)}), bf16[64,32,1024]{2,1,0:T(8,128)(2,1)}, u32[]{:S(2)}, u32[]{:S(2)}) async-start(bf16[64,32,1024]{2,1,0:T(8,128)(2,1)} %bitcast_select_fusion), calls=%async_computation | async-start | bytes 8388608 | tf_op jit(solution)/shard_map/all_to_all | solution.py:77
  34.7 183.0 %all-to-all-done = bf16[64,32,1024]{2,1,0:T(8,128)(2,1)} async-done(((bf16[64,32,1024]{2,1,0:T(8,128)(2,1)}), bf16[64,32,1024]{2,1,0:T(8,128)(2,1)}, u32[]{:S(2)}, u32[]{:S(2)}) %all-to-all-start) | async-done | bytes 4194336 | tf_op jit(solution)/shard_map/all_to_all | solution.py:77
  217.7 3.1 slice_bitcast_fusion
  220.8 1.0 copy.44
  221.8 1.4 fusion.23
  223.2 5.1 %fusion.38 = (f32[8,1024]{1,0:T(8,128)S(1)}, f32[8,1024,192]{1,2,0:T(8,128)S(1)}) fusion(f32[8,1024,192]{1,2,0:T(8,128)S(1)} %fusion.23), kind=kOutput, calls=%fused_computation.64 | output fusion | flops 6291647 | bytes 12615680 | tf_op jit(solution)/shard_map/sub | solution.py:28
  228.3 0.6 copy.46
  229.0 1.0 fusion.7
  230.0 2.3 multiply_reduce_fusion.1
  232.3 2.3 multiply_convert_fusion
  234.7 2.0 fusion.8
  236.7 2.7 copy.40
  239.4 4.2 reshape_reshape.3
  243.8 3.9 pad_maximum_fusion
  247.7 16.5 %all-to-all-start.1 = ((bf16[64,18,1024]{2,1,0:T(8,128)(2,1)}), bf16[64,18,1024]{2,1,0:T(8,128)(2,1)}, u32[]{:S(2)}, u32[]{:S(2)}) async-start(bf16[64,18,1024]{2,1,0:T(8,128)(2,1)} %pad_maximum_fusion), calls=%async_computation.1 | async-start | bytes 6291456 | tf_op jit(solution)/shard_map/all_to_all | solution.py:87
  264.4 3.7 fusion.18
  268.4 0.9 broadcast_in_dim_reshape.6
  269.3 3.7 fusion.19
  273.3 0.9 broadcast_in_dim_reshape.7
  274.2 130.0 %all-to-all-done.1 = bf16[64,18,1024]{2,1,0:T(8,128)(2,1)} async-done(((bf16[64,18,1024]{2,1,0:T(8,128)(2,1)}), bf16[64,18,1024]{2,1,0:T(8,128)(2,1)}, u32[]{:S(2)}, u32[]{:S(2)}) %all-to-all-start.1) | async-done | bytes 2359328 | tf_op jit(solution)/shard_map/all_to_all | solution.py:87
  404.2 1.5 convert_reduce_fusion
  405.7 22.8 %psum.7 = f32[1024]{0:T(1024)} all-reduce(f32[1024]{0:T(1024)S(1)} %convert_reduce_fusion), channel_id=1, replica_groups=mesh['grp'=8,'spec'=64] {'grp'}, use_global_device_ids=true, to_apply=%region_9.10 | all-reduce | flops 1024 | bytes 8192 | tf_op jit(solution)/shard_map/psum | solution.py:89
  428.6 1.8 slice.22
  430.3 0.6 gather_fusion.1
  431.0 1.1 bitcast_select_fusion.1
  (36 shorter events, 1.6 us)
Async XLA Ops:
  12.4 22.1 %copy-start.3 = (bf16[1,192,1024]{2,1,0:T(8,128)(2,1)S(1)}, bf16[1,192,1024]{2,1,0:T(8,128)(2,1)}, u32[]{:S(2)}) copy-start(bf16[1,192,1024]{2,1,0:T(8,128)(2,1)} %param.8) | copy-start | bytes 1179652
  12.4 22.2 %copy-start.4 = (bf16[1,192,1024]{2,1,0:T(8,128)(2,1)S(1)}, bf16[1,192,1024]{2,1,0:T(8,128)(2,1)}, u32[]{:S(2)}) copy-start(bf16[1,192,1024]{2,1,0:T(8,128)(2,1)} %param.9) | copy-start | bytes 1179652
  12.4 22.3 %copy-start.6 = (f32[1024]{0:T(1024)S(1)}, f32[1024]{0:T(1024)}, u32[]{:S(2)}) copy-start(f32[1024]{0:T(1024)} %param.11) | copy-start | bytes 12292
  12.4 205.3 %all-to-all-start = ((bf16[64,32,1024]{2,1,0:T(8,128)(2,1)}), bf16[64,32,1024]{2,1,0:T(8,128)(2,1)}, u32[]{:S(2)}, u32[]{:S(2)}) async-start(bf16[64,32,1024]{2,1,0:T(8,128)(2,1)} %bitcast_select_fusion), calls=%async_computation | async-start | bytes 8388608 | tf_op jit(solution)/shard_map/all_to_all | solution.py:77
  34.7 195.3 %copy-start.5 = (bf16[24,8,8,128]{3,2,1,0:T(8,128)(2,1)}, bf16[24,8,8,128]{3,2,1,0:T(8,128)(2,1)S(1)}, u32[]{:S(2)}) copy-start(bf16[24,8,8,128]{3,2,1,0:T(8,128)(2,1)S(1)} %copy.47) | copy-start | bytes 1179652
  221.8 12.9 %copy-start = (f32[128,8,8,128]{3,2,1,0:T(8,128)}, f32[128,8,8,128]{3,2,1,0:T(8,128)S(1)}, u32[]{:S(2)}) copy-start(f32[128,8,8,128]{3,2,1,0:T(8,128)S(1)} %copy.44) | copy-start | bytes 12582916
  228.9 3.3 copy-start.2
  230.0 4.7 %copy-start.1 = (bf16[8,1024,192]{1,2,0:T(8,128)(2,1)}, bf16[8,1024,192]{1,2,0:T(8,128)(2,1)S(1)}, u32[]{:S(2)}) copy-start(bf16[8,1024,192]{1,2,0:T(8,128)(2,1)S(1)} %fusion.7) | copy-start | bytes 9437188
  247.7 16.6 %copy-start.7 = (s32[64,1]{0,1:T(1,128)S(1)}, s32[64,1]{0,1:T(1,128)}, u32[]{:S(2)}) copy-start(s32[64,1]{0,1:T(1,128)} %param.10) | copy-start | bytes 772
  247.7 156.6 %all-to-all-start.1 = ((bf16[64,18,1024]{2,1,0:T(8,128)(2,1)}), bf16[64,18,1024]{2,1,0:T(8,128)(2,1)}, u32[]{:S(2)}, u32[]{:S(2)}) async-start(bf16[64,18,1024]{2,1,0:T(8,128)(2,1)} %pad_maximum_fusion), calls=%async_computation.1 | async-start | bytes 6291456 | tf_op jit(solution)/shard_map/all_to_all | solution.py:87

commit v5 on v4

--- a/solution.py
+++ b/solution.py
@@ -71,8 +71,9 @@
         [queries.reshape(cand_count, qtok_here, width), out_grad.reshape(cand_count, qtok_here, width)],
         axis=1,
     )
+    both = jnp.pad(both, ((0, 1), (0, 0), (0, 0)))
     source = jnp.where(used, source, cand_count)
-    send_both = jnp.take(both, source, axis=0, mode="fill", fill_value=0)
+    send_both = jnp.take(both, source, axis=0, mode="clip")
     send_both = send_both.reshape(peers, CAP * 2 * qtok_here, width)
     recv_both = lax.all_to_all(send_both, "spec", split_axis=0, concat_axis=0, tiled=True)
     recv_both = recv_both.reshape(slot_count, 2, qtok_here, width)
@@ -88,7 +89,9 @@
     spec_sum = jnp.sum(came_back[:, CAP * qtok_here :].astype(jnp.float32), axis=(0, 1))
     gain_grad = lax.psum(spec_sum, "grp")
     came_back = came_back[:, : CAP * qtok_here]
-    home_grads = jnp.take(came_back.reshape(slot_count, qtok_here, width), slot_index, axis=0)
+    home_grads = jnp.take(
+        came_back.reshape(slot_count, qtok_here, width), slot_index, axis=0, mode="clip"
+    )
     query_grad = home_grads.reshape(cand_count * qtok_here, width)
     return (
         query_grad,

time: 433 us -> 428 us (0.988)
  other arithmetic: 24.2 us -> 19.3 us
    select_n x2 -> x1, other arithmetic: 4.88 us -> 0.01 us  [shards(): source = jnp.where(used, source, cand_count)]
where the time goes in v5:
time: 428 us; the launch traced here: 427 us
  waiting for transfers between devices  314 us (73%)
  starting transfers between devices  38.7 us (9%)
  blocking collectives  21.7 us (5%)
  other arithmetic  19.3 us (5%)
  local copies, waits for them, and re-layouts  17.4 us (4%)
  matrix products  15.4 us (4%)
    all_to_all x1, waiting for transfers between devices, shards(): lax.all_to_all(send_both, 'spec', split_axis=0, concat_axis=0, tiled=True)  183 us
    all_to_all x1, waiting for transfers between devices, shards(): lax.all_to_all(going_back, 'spec', split_axis=0, concat_axis=0, tiled=True)  131 us
    all_to_all x1, starting transfers between devices, shards(): lax.all_to_all(send_both, 'spec', split_axis=0, concat_axis=0, tiled=True)  22.1 us
    psum x1, blocking collectives, shards(): gain_grad = lax.psum(spec_sum, 'grp')  21.7 us
    all_to_all x1, starting transfers between devices, shards(): lax.all_to_all(going_back, 'spec', split_axis=0, concat_axis=0, tiled=True)  16.5 us
  transfers between devices with their start and end apart: 2, of which 2 were waited for; matrix products, arithmetic and copies ran while one was open for 2% of the time, Pallas kernels for 0%

profile of v5, /device:TPU:1, one launch (start us, length us, event | category | flops | bytes accessed | tf_op | source)
XLA Modules:
  0.0 427.4 jit_solution(15836815978755692351)
XLA Ops:
  0.6 0.7 fusion.37
  1.5 0.8 select_reduce_fusion
  2.3 0.7 multiply_add_fusion
  3.0 0.6 iota_reduce_fusion
  3.7 1.8 fusion.10
  5.5 2.8 gather_fusion
  8.3 22.1 %all-to-all-start = ((bf16[64,32,1024]{2,1,0:T(8,128)(2,1)}), bf16[64,32,1024]{2,1,0:T(8,128)(2,1)}, u32[]{:S(2)}, u32[]{:S(2)}) async-start(bf16[64,32,1024]{2,1,0:T(8,128)(2,1)} %bitcast.77), calls=%async_computation | async-start | bytes 8388608 | tf_op jit(solution)/shard_map/all_to_all | solution.py:78
  30.6 183.0 %all-to-all-done = bf16[64,32,1024]{2,1,0:T(8,128)(2,1)} async-done(((bf16[64,32,1024]{2,1,0:T(8,128)(2,1)}), bf16[64,32,1024]{2,1,0:T(8,128)(2,1)}, u32[]{:S(2)}, u32[]{:S(2)}) %all-to-all-start) | async-done | bytes 4194336 | tf_op jit(solution)/shard_map/all_to_all | solution.py:78
  213.6 3.1 slice_bitcast_fusion
  216.6 1.0 copy.38
  217.7 1.4 fusion.26
  219.1 5.1 %fusion.42 = (f32[8,1024]{1,0:T(8,128)S(1)}, f32[8,1024,192]{1,2,0:T(8,128)S(1)}) fusion(f32[8,1024,192]{1,2,0:T(8,128)S(1)} %fusion.26), kind=kOutput, calls=%fused_computation.63 | output fusion | flops 6291647 | bytes 12615680 | tf_op jit(solution)/shard_map/sub | solution.py:28
  224.2 0.6 copy.40
  224.8 1.0 fusion.9
  225.8 2.3 multiply_reduce_fusion.1
  228.2 2.3 multiply_convert_fusion
  230.5 2.0 fusion.11
  232.5 2.7 copy.34
  235.3 4.2 reshape_reshape.3
  239.7 3.9 pad_maximum_fusion
  243.5 16.5 %all-to-all-start.1 = ((bf16[64,18,1024]{2,1,0:T(8,128)(2,1)}), bf16[64,18,1024]{2,1,0:T(8,128)(2,1)}, u32[]{:S(2)}, u32[]{:S(2)}) async-start(bf16[64,18,1024]{2,1,0:T(8,128)(2,1)} %pad_maximum_fusion), calls=%async_computation.1 | async-start | bytes 6291456 | tf_op jit(solution)/shard_map/all_to_all | solution.py:88
  260.1 3.6 fusion.21
  263.8 0.3 copy.35
  264.0 0.9 broadcast_in_dim_reshape.6
  265.0 3.7 fusion.22
  268.7 0.3 copy.36
  269.0 0.9 broadcast_in_dim_reshape.7
  269.9 131.0 %all-to-all-done.1 = bf16[64,18,1024]{2,1,0:T(8,128)(2,1)} async-done(((bf16[64,18,1024]{2,1,0:T(8,128)(2,1)}), bf16[64,18,1024]{2,1,0:T(8,128)(2,1)}, u32[]{:S(2)}, u32[]{:S(2)}) %all-to-all-start.1) | async-done | bytes 2359328 | tf_op jit(solution)/shard_map/all_to_all | solution.py:88
  400.8 1.5 convert_reduce_fusion
  402.3 21.7 %psum.7 = f32[1024]{0:T(1024)} all-reduce(f32[1024]{0:T(1024)S(1)} %convert_reduce_fusion), channel_id=1, replica_groups=mesh['grp'=8,'spec'=64] {'grp'}, use_global_device_ids=true, to_apply=%region_9.10 | all-reduce | flops 1024 | bytes 8192 | tf_op jit(solution)/shard_map/psum | solution.py:90
  424.0 1.8 slice.22
  425.8 1.6 gather_fusion.1
  (28 shorter events, 0.5 us)
Async XLA Ops:
  8.3 22.1 %copy-start.3 = (bf16[1,192,1024]{2,1,0:T(8,128)(2,1)S(1)}, bf16[1,192,1024]{2,1,0:T(8,128)(2,1)}, u32[]{:S(2)}) copy-start(bf16[1,192,1024]{2,1,0:T(8,128)(2,1)} %param.8) | copy-start | bytes 1179652
  8.3 22.2 %copy-start.4 = (bf16[1,192,1024]{2,1,0:T(8,128)(2,1)S(1)}, bf16[1,192,1024]{2,1,0:T(8,128)(2,1)}, u32[]{:S(2)}) copy-start(bf16[1,192,1024]{2,1,0:T(8,128)(2,1)} %param.9) | copy-start | bytes 1179652
  8.3 22.3 %copy-start.6 = (f32[1024]{0:T(1024)S(1)}, f32[1024]{0:T(1024)}, u32[]{:S(2)}) copy-start(f32[1024]{0:T(1024)} %param.11) | copy-start | bytes 12292
  8.3 205.3 %all-to-all-start = ((bf16[64,32,1024]{2,1,0:T(8,128)(2,1)}), bf16[64,32,1024]{2,1,0:T(8,128)(2,1)}, u32[]{:S(2)}, u32[]{:S(2)}) async-start(bf16[64,32,1024]{2,1,0:T(8,128)(2,1)} %bitcast.77), calls=%async_computation | async-start | bytes 8388608 | tf_op jit(solution)/shard_map/all_to_all | solution.py:78
  30.6 195.3 %copy-start.5 = (bf16[24,8,8,128]{3,2,1,0:T(8,128)(2,1)}, bf16[24,8,8,128]{3,2,1,0:T(8,128)(2,1)S(1)}, u32[]{:S(2)}) copy-start(bf16[24,8,8,128]{3,2,1,0:T(8,128)(2,1)S(1)} %copy.41) | copy-start | bytes 1179652
  217.7 12.9 %copy-start = (f32[128,8,8,128]{3,2,1,0:T(8,128)}, f32[128,8,8,128]{3,2,1,0:T(8,128)S(1)}, u32[]{:S(2)}) copy-start(f32[128,8,8,128]{3,2,1,0:T(8,128)S(1)} %copy.38) | copy-start | bytes 12582916
  224.8 3.3 copy-start.2
  225.8 4.7 %copy-start.1 = (bf16[8,1024,192]{1,2,0:T(8,128)(2,1)}, bf16[8,1024,192]{1,2,0:T(8,128)(2,1)S(1)}, u32[]{:S(2)}) copy-start(bf16[8,1024,192]{1,2,0:T(8,128)(2,1)S(1)} %fusion.9) | copy-start | bytes 9437188
  243.5 16.5 %copy-start.7 = (s32[64,1]{0,1:T(1,128)S(1)}, s32[64,1]{0,1:T(1,128)}, u32[]{:S(2)}) copy-start(s32[64,1]{0,1:T(1,128)} %param.10) | copy-start | bytes 772
  243.5 157.3 %all-to-all-start.1 = ((bf16[64,18,1024]{2,1,0:T(8,128)(2,1)}), bf16[64,18,1024]{2,1,0:T(8,128)(2,1)}, u32[]{:S(2)}, u32[]{:S(2)}) async-start(bf16[64,18,1024]{2,1,0:T(8,128)(2,1)} %pad_maximum_fusion), calls=%async_computation.1 | async-start | bytes 6291456 | tf_op jit(solution)/shard_map/all_to_all | solution.py:88

commit v6 on v5

--- a/solution.py
+++ b/solution.py
@@ -36,7 +36,7 @@
     k_grad = jnp.einsum("hrk,hrd->hkd", dscores, gained_hm, preferred_element_type=f32) * inv_root
     v_grad = jnp.einsum("hrk,hrd->hkd", probs_b, g_hm, preferred_element_type=f32)
     gain_part = jnp.sum(raw_hm.astype(f32) * q_grad, axis=1).reshape(width)
-    going_back = (q_grad * gain_hm).astype(jnp.bfloat16).transpose(1, 0, 2).reshape(total_rows, width)
+    going_back = (q_grad * gain_hm).astype(jnp.bfloat16).transpose(1, 0, 2)
     key_grad = k_grad.astype(jnp.bfloat16).transpose(1, 0, 2).reshape(key_count, width)
     value_grad = v_grad.astype(jnp.bfloat16).transpose(1, 0, 2).reshape(key_count, width)
     return (going_back, gain_part, key_grad, value_grad)
@@ -82,15 +82,18 @@
     going_back, partial_value, key_grad, value_grad = attend_backward(
         recv_rows, recv_cotan, spec_keys[0], spec_values[0], query_gain
     )
-    going_back = going_back.reshape(peers, CAP * qtok_here, width)
-    gain_rows = jnp.broadcast_to(split_pieces(partial_value, PIECES)[None], (peers, PIECES, width))
+    going_back = going_back.reshape(peers, CAP * qtok_here, HEADS, width // HEADS)
+    gain_rows = jnp.broadcast_to(
+        split_pieces(partial_value, PIECES).reshape(1, PIECES, HEADS, width // HEADS),
+        (peers, PIECES, HEADS, width // HEADS),
+    )
     going_back = jnp.concatenate([going_back, gain_rows], axis=1)
     came_back = lax.all_to_all(going_back, "spec", split_axis=0, concat_axis=0, tiled=True)
-    spec_sum = jnp.sum(came_back[:, CAP * qtok_here :].astype(jnp.float32), axis=(0, 1))
+    spec_sum = jnp.sum(came_back[:, CAP * qtok_here :].astype(jnp.float32), axis=(0, 1)).reshape(width)
     gain_grad = lax.psum(spec_sum, "grp")
     came_back = came_back[:, : CAP * qtok_here]
     home_grads = jnp.take(
-        came_back.reshape(slot_count, qtok_here, width), slot_index, axis=0, mode="clip"
+        came_back.reshape(slot_count, qtok_here, HEADS, width // HEADS), slot_index, axis=0, mode="clip"
     )
     query_grad = home_grads.reshape(cand_count * qtok_here, width)
     return (

time: 428 us -> 386 us (0.902)
  waiting for transfers between devices: 314 us -> 280 us
  local copies, waits for them, and re-layouts: 17.4 us -> 13.1 us
    all_to_all x1, waiting for transfers between devices: 131 us -> 96.8 us  [shards(): lax.all_to_all(going_back, 'spec', split_axis=0, concat_axis=0, tiled=True)]
  transfers between devices with their start and end apart: 2 -> 2, of which waited for: 2 -> 2; matrix products, arithmetic and copies ran while one was open for 2% -> 3% of each run, Pallas kernels for 0% -> 0%
where the time goes in v6:
time: 386 us
  waiting for transfers between devices  280 us (73%)
  starting transfers between devices  38.8 us (10%)
  blocking collectives  20.9 us (5%)
  other arithmetic  16.9 us (4%)
  matrix products  15.4 us (4%)
  local copies, waits for them, and re-layouts  13.1 us (3%)
    all_to_all x1, waiting for transfers between devices, shards(): lax.all_to_all(send_both, 'spec', split_axis=0, concat_axis=0, tiled=True)  183 us
    all_to_all x1, waiting for transfers between devices, shards(): lax.all_to_all(going_back, 'spec', split_axis=0, concat_axis=0, tiled=True)  96.8 us
    all_to_all x1, starting transfers between devices, shards(): lax.all_to_all(send_both, 'spec', split_axis=0, concat_axis=0, tiled=True)  22.1 us
    psum x1, blocking collectives, shards(): gain_grad = lax.psum(spec_sum, 'grp')  20.9 us
    all_to_all x1, starting transfers between devices, shards(): lax.all_to_all(going_back, 'spec', split_axis=0, concat_axis=0, tiled=True)  16.6 us
  transfers between devices with their start and end apart: 2, of which 2 were waited for; matrix products, arithmetic and copies ran while one was open for 3% of the time, Pallas kernels for 0%

profile of v6, /device:TPU:1, one launch (start us, length us, event | category | flops | bytes accessed | tf_op | source)
XLA Modules:
  0.0 385.8 jit_solution(9436022359792061100)
XLA Ops:
  0.6 0.7 fusion.36
  1.5 0.8 select_reduce_fusion
  2.3 0.7 multiply_add_fusion
  3.0 0.6 iota_reduce_fusion
  3.7 1.8 fusion.10
  5.5 2.8 gather_fusion
  8.3 22.1 %all-to-all-start = ((bf16[64,32,1024]{2,1,0:T(8,128)(2,1)}), bf16[64,32,1024]{2,1,0:T(8,128)(2,1)}, u32[]{:S(2)}, u32[]{:S(2)}) async-start(bf16[64,32,1024]{2,1,0:T(8,128)(2,1)} %bitcast.85), calls=%async_computation | async-start | bytes 8388608 | tf_op jit(solution)/shard_map/all_to_all | solution.py:78
  30.6 183.0 %all-to-all-done = bf16[64,32,1024]{2,1,0:T(8,128)(2,1)} async-done(((bf16[64,32,1024]{2,1,0:T(8,128)(2,1)}), bf16[64,32,1024]{2,1,0:T(8,128)(2,1)}, u32[]{:S(2)}, u32[]{:S(2)}) %all-to-all-start) | async-done | bytes 4194336 | tf_op jit(solution)/shard_map/all_to_all | solution.py:78
  213.6 3.1 slice_bitcast_fusion
  216.7 1.0 copy.44
  217.7 1.4 fusion.25
  219.1 5.3 %fusion.41 = (f32[8,1024]{1,0:T(8,128)S(1)}, f32[8,1024,192]{1,2,0:T(8,128)S(1)}) fusion(f32[8,1024,192]{1,2,0:T(8,128)S(1)} %fusion.25), kind=kOutput, calls=%fused_computation.63 | output fusion | flops 6291647 | bytes 12615680 | tf_op jit(solution)/shard_map/sub | solution.py:28
  224.4 0.6 copy.46
  225.0 1.0 fusion.9
  226.0 2.3 multiply_reduce_fusion.1
  228.4 2.3 multiply_convert_fusion
  230.7 2.0 multiply_convert_fusion.1
  232.7 2.4 copy.40
  235.2 1.6 pad_maximum_fusion
  236.9 16.6 %all-to-all-start.1 = ((bf16[64,18,8,128]{3,2,1,0:T(8,128)(2,1)}), bf16[64,18,8,128]{3,2,1,0:T(8,128)(2,1)}, u32[]{:S(2)}, u32[]{:S(2)}) async-start(bf16[64,18,8,128]{3,2,1,0:T(8,128)(2,1)} %pad_maximum_fusion), calls=%async_computation.1 | async-start | bytes 4718592 | tf_op jit(solution)/shard_map/all_to_all | solution.py:91
  253.5 3.6 fusion.20
  257.2 0.3 copy.41
  257.4 0.9 broadcast_in_dim_reshape.6
  258.4 3.7 fusion.21
  262.1 0.3 copy.42
  262.4 0.9 broadcast_in_dim_reshape.7
  263.3 96.8 %all-to-all-done.1 = bf16[64,18,8,128]{3,2,1,0:T(8,128)(2,1)} async-done(((bf16[64,18,8,128]{3,2,1,0:T(8,128)(2,1)}), bf16[64,18,8,128]{3,2,1,0:T(8,128)(2,1)}, u32[]{:S(2)}, u32[]{:S(2)}) %all-to-all-start.1) | async-done | bytes 2359328 | tf_op jit(solution)/shard_map/all_to_all | solution.py:91
  360.1 1.7 slice.22
  361.8 0.7 gather_fusion.1
  362.6 1.2 copy.85
  363.8 1.1 convert_reduce_fusion
  364.9 20.9 %psum.7 = f32[1024]{0:T(1024)} all-reduce(f32[1024]{0:T(1024)S(1)} %bitcast.102), channel_id=1, replica_groups=mesh['grp'=8,'spec'=64] {'grp'}, use_global_device_ids=true, to_apply=%region_9.10 | all-reduce | flops 1024 | bytes 8192 | tf_op jit(solution)/shard_map/psum | solution.py:93
  (28 shorter events, 0.4 us)
Async XLA Ops:
  8.3 22.1 %copy-start.3 = (bf16[1,192,1024]{2,1,0:T(8,128)(2,1)S(1)}, bf16[1,192,1024]{2,1,0:T(8,128)(2,1)}, u32[]{:S(2)}) copy-start(bf16[1,192,1024]{2,1,0:T(8,128)(2,1)} %param.8) | copy-start | bytes 1179652
  8.3 22.2 %copy-start.4 = (bf16[1,192,1024]{2,1,0:T(8,128)(2,1)S(1)}, bf16[1,192,1024]{2,1,0:T(8,128)(2,1)}, u32[]{:S(2)}) copy-start(bf16[1,192,1024]{2,1,0:T(8,128)(2,1)} %param.9) | copy-start | bytes 1179652
  8.3 22.3 %copy-start.6 = (f32[1024]{0:T(1024)S(1)}, f32[1024]{0:T(1024)}, u32[]{:S(2)}) copy-start(f32[1024]{0:T(1024)} %param.11) | copy-start | bytes 12292
  8.3 205.3 %all-to-all-start = ((bf16[64,32,1024]{2,1,0:T(8,128)(2,1)}), bf16[64,32,1024]{2,1,0:T(8,128)(2,1)}, u32[]{:S(2)}, u32[]{:S(2)}) async-start(bf16[64,32,1024]{2,1,0:T(8,128)(2,1)} %bitcast.85), calls=%async_computation | async-start | bytes 8388608 | tf_op jit(solution)/shard_map/all_to_all | solution.py:78
  30.6 195.5 %copy-start.5 = (bf16[24,8,8,128]{3,2,1,0:T(8,128)(2,1)}, bf16[24,8,8,128]{3,2,1,0:T(8,128)(2,1)S(1)}, u32[]{:S(2)}) copy-start(bf16[24,8,8,128]{3,2,1,0:T(8,128)(2,1)S(1)} %copy.47) | copy-start | bytes 1179652
  217.7 13.0 %copy-start = (f32[128,8,8,128]{3,2,1,0:T(8,128)}, f32[128,8,8,128]{3,2,1,0:T(8,128)S(1)}, u32[]{:S(2)}) copy-start(f32[128,8,8,128]{3,2,1,0:T(8,128)S(1)} %copy.44) | copy-start | bytes 12582916
  225.0 3.3 copy-start.2
  226.0 4.7 %copy-start.1 = (bf16[8,1024,192]{1,2,0:T(8,128)(2,1)}, bf16[8,1024,192]{1,2,0:T(8,128)(2,1)S(1)}, u32[]{:S(2)}) copy-start(bf16[8,1024,192]{1,2,0:T(8,128)(2,1)S(1)} %fusion.9) | copy-start | bytes 9437188
  235.2 18.3 %copy-start.7 = (s32[64,1]{0,1:T(1,128)S(1)}, s32[64,1]{0,1:T(1,128)}, u32[]{:S(2)}) copy-start(s32[64,1]{0,1:T(1,128)} %param.10) | copy-start | bytes 772
  236.9 123.2 %all-to-all-start.1 = ((bf16[64,18,8,128]{3,2,1,0:T(8,128)(2,1)}), bf16[64,18,8,128]{3,2,1,0:T(8,128)(2,1)}, u32[]{:S(2)}, u32[]{:S(2)}) async-start(bf16[64,18,8,128]{3,2,1,0:T(8,128)(2,1)} %pad_maximum_fusion), calls=%async_computation.1 | async-start | bytes 4718592 | tf_op jit(solution)/shard_map/all_to_all | solution.py:91

commit v7 on v6

--- a/solution.py
+++ b/solution.py
@@ -12,14 +12,14 @@
 
 
 def attend_backward(recv_rows, recv_grads, keys_here, values_here, query_gain):
-    total_rows, width = recv_rows.shape
-    head_dim = width // HEADS
+    total_rows, _, head_dim = recv_rows.shape
+    width = HEADS * head_dim
     key_count = keys_here.shape[0]
     inv_root = 1.0 / math.sqrt(HEAD_DIM)
     f32 = jnp.float32
     gain_hm = query_gain.reshape(HEADS, 1, head_dim)
-    raw_hm = recv_rows.reshape(total_rows, HEADS, head_dim).transpose(1, 0, 2)
-    g_hm = recv_grads.reshape(total_rows, HEADS, head_dim).transpose(1, 0, 2)
+    raw_hm = recv_rows.transpose(1, 0, 2)
+    g_hm = recv_grads.transpose(1, 0, 2)
     k_hm = keys_here.reshape(key_count, HEADS, head_dim).transpose(1, 0, 2)
     v_hm = values_here.reshape(key_count, HEADS, head_dim).transpose(1, 0, 2)
     gained_hm = (raw_hm.astype(f32) * gain_hm).astype(jnp.bfloat16)
@@ -67,18 +67,22 @@
     matches = jnp.arange(slot_count, dtype=jnp.int32)[:, None] == slot_index[None, :]
     source = jnp.argmax(matches, axis=1).astype(jnp.int32)
     used = jnp.any(matches, axis=1)
+    head_dim = width // HEADS
     both = jnp.concatenate(
-        [queries.reshape(cand_count, qtok_here, width), out_grad.reshape(cand_count, qtok_here, width)],
+        [
+            queries.reshape(cand_count, qtok_here, HEADS, head_dim),
+            out_grad.reshape(cand_count, qtok_here, HEADS, head_dim),
+        ],
         axis=1,
     )
-    both = jnp.pad(both, ((0, 1), (0, 0), (0, 0)))
+    both = jnp.pad(both, ((0, 1), (0, 0), (0, 0), (0, 0)))
     source = jnp.where(used, source, cand_count)
     send_both = jnp.take(both, source, axis=0, mode="clip")
-    send_both = send_both.reshape(peers, CAP * 2 * qtok_here, width)
+    send_both = send_both.reshape(peers, CAP * 2 * qtok_here, HEADS, head_dim)
     recv_both = lax.all_to_all(send_both, "spec", split_axis=0, concat_axis=0, tiled=True)
-    recv_both = recv_both.reshape(slot_count, 2, qtok_here, width)
-    recv_rows = recv_both[:, 0].reshape(slot_count * qtok_here, width)
-    recv_cotan = recv_both[:, 1].reshape(slot_count * qtok_here, width)
+    recv_both = recv_both.reshape(slot_count, 2, qtok_here, HEADS, head_dim)
+    recv_rows = recv_both[:, 0].reshape(slot_count * qtok_here, HEADS, head_dim)
+    recv_cotan = recv_both[:, 1].reshape(slot_count * qtok_here, HEADS, head_dim)
     going_back, partial_value, key_grad, value_grad = attend_backward(
         recv_rows, recv_cotan, spec_keys[0], spec_values[0], query_gain
     )

time: 386 us -> 386 us (level)
  no operation moved by 1% of the time
where the time goes in v7:
time: 386 us; the launch traced here: 385 us
  waiting for transfers between devices  281 us (73%)
  starting transfers between devices  37.5 us (10%)
  blocking collectives  21 us (5%)
  matrix products  15.4 us (4%)
  other arithmetic  15.1 us (4%)
  local copies, waits for them, and re-layouts  13.9 us (4%)
    all_to_all x1, waiting for transfers between devices, shards(): lax.all_to_all(send_both, 'spec', split_axis=0, concat_axis=0, tiled=True)  184 us
    all_to_all x1, waiting for transfers between devices, shards(): lax.all_to_all(going_back, 'spec', split_axis=0, concat_axis=0, tiled=True)  96.9 us
    all_to_all x1, starting transfers between devices, shards(): lax.all_to_all(send_both, 'spec', split_axis=0, concat_axis=0, tiled=True)  22.3 us
    psum x1, blocking collectives, shards(): gain_grad = lax.psum(spec_sum, 'grp')  21 us
    all_to_all x1, starting transfers between devices, shards(): lax.all_to_all(going_back, 'spec', split_axis=0, concat_axis=0, tiled=True)  15.2 us
  transfers between devices with their start and end apart: 2, of which 2 were waited for; matrix products, arithmetic and copies ran while one was open for 3% of the time, Pallas kernels for 0%

profile of v7, /device:TPU:1, one launch (start us, length us, event | category | flops | bytes accessed | tf_op | source)
XLA Modules:
  0.0 385.1 jit_solution(2665026931376670259)
XLA Ops:
  0.6 0.7 fusion.36
  1.4 0.1 reduce_window_sum.11
  1.5 0.8 select_reduce_fusion
  2.3 0.7 multiply_add_fusion
  3.0 0.6 iota_reduce_fusion
  3.7 2.2 copy_bitcast_fusion.1
  5.9 0.2 fusion.10
  6.1 3.1 gather_fusion
  9.1 22.3 %all-to-all-start = ((bf16[64,32,8,128]{3,2,1,0:T(8,128)(2,1)}), bf16[64,32,8,128]{3,2,1,0:T(8,128)(2,1)}, u32[]{:S(2)}, u32[]{:S(2)}) async-start(bf16[64,32,8,128]{3,2,1,0:T(8,128)(2,1)} %bitcast.82), calls=%async_computation | async-start | bytes 8388608 | tf_op jit(solution)/shard_map/all_to_all | solution.py:82
  31.6 184.3 %all-to-all-done = bf16[64,32,8,128]{3,2,1,0:T(8,128)(2,1)} async-done(((bf16[64,32,8,128]{3,2,1,0:T(8,128)(2,1)}), bf16[64,32,8,128]{3,2,1,0:T(8,128)(2,1)}, u32[]{:S(2)}, u32[]{:S(2)}) %all-to-all-start) | async-done | bytes 4194336 | tf_op jit(solution)/shard_map/all_to_all | solution.py:82
  215.9 3.1 fusion.41
  219.0 1.4 fusion.25
  220.4 5.1 %fusion.42 = (f32[8,1024]{1,0:T(8,128)S(1)}, f32[8,1024,192]{1,2,0:T(8,128)S(1)}) fusion(f32[8,1024,192]{1,2,0:T(8,128)S(1)} %fusion.25), kind=kOutput, calls=%fused_computation.65 | output fusion | flops 6291647 | bytes 12615680 | tf_op jit(solution)/shard_map/sub | solution.py:28
  225.5 1.0 fusion.9
  226.5 2.3 multiply_reduce_fusion.1
  228.9 2.3 multiply_convert_fusion
  231.2 2.0 multiply_convert_fusion.1
  233.2 2.4 copy.40
  235.8 1.6 pad_maximum_fusion
  237.4 15.2 %all-to-all-start.1 = ((bf16[64,18,8,128]{3,2,1,0:T(8,128)(2,1)}), bf16[64,18,8,128]{3,2,1,0:T(8,128)(2,1)}, u32[]{:S(2)}, u32[]{:S(2)}) async-start(bf16[64,18,8,128]{3,2,1,0:T(8,128)(2,1)} %pad_maximum_fusion), calls=%async_computation.1 | async-start | bytes 4718592 | tf_op jit(solution)/shard_map/all_to_all | solution.py:95
  252.6 3.6 fusion.20
  256.2 0.3 copy.41
  256.5 0.9 broadcast_in_dim_reshape.6
  257.4 3.7 fusion.21
  261.1 0.3 copy.42
  261.4 0.9 broadcast_in_dim_reshape.7
  262.3 96.9 %all-to-all-done.1 = bf16[64,18,8,128]{3,2,1,0:T(8,128)(2,1)} async-done(((bf16[64,18,8,128]{3,2,1,0:T(8,128)(2,1)}), bf16[64,18,8,128]{3,2,1,0:T(8,128)(2,1)}, u32[]{:S(2)}, u32[]{:S(2)}) %all-to-all-start.1) | async-done | bytes 2359328 | tf_op jit(solution)/shard_map/all_to_all | solution.py:95
  359.2 1.7 slice.22
  360.9 0.7 gather_fusion.1
  361.7 1.2 copy.87
  362.9 1.1 convert_reduce_fusion
  364.0 21.0 %psum.7 = f32[1024]{0:T(1024)} all-reduce(f32[1024]{0:T(1024)S(1)} %bitcast.96), channel_id=1, replica_groups=mesh['grp'=8,'spec'=64] {'grp'}, use_global_device_ids=true, to_apply=%region_9.10 | all-reduce | flops 1024 | bytes 8192 | tf_op jit(solution)/shard_map/psum | solution.py:97
  (27 shorter events, 0.3 us)
Async XLA Ops:
  9.1 22.3 %copy-start.3 = (bf16[1,192,1024]{2,1,0:T(8,128)(2,1)S(1)}, bf16[1,192,1024]{2,1,0:T(8,128)(2,1)}, u32[]{:S(2)}) copy-start(bf16[1,192,1024]{2,1,0:T(8,128)(2,1)} %param.8) | copy-start | bytes 1179652
  9.1 22.4 %copy-start.4 = (bf16[1,192,1024]{2,1,0:T(8,128)(2,1)S(1)}, bf16[1,192,1024]{2,1,0:T(8,128)(2,1)}, u32[]{:S(2)}) copy-start(bf16[1,192,1024]{2,1,0:T(8,128)(2,1)} %param.9) | copy-start | bytes 1179652
  9.1 22.5 %copy-start.6 = (f32[1024]{0:T(1024)S(1)}, f32[1024]{0:T(1024)}, u32[]{:S(2)}) copy-start(f32[1024]{0:T(1024)} %param.11) | copy-start | bytes 12292
  9.1 206.8 %all-to-all-start = ((bf16[64,32,8,128]{3,2,1,0:T(8,128)(2,1)}), bf16[64,32,8,128]{3,2,1,0:T(8,128)(2,1)}, u32[]{:S(2)}, u32[]{:S(2)}) async-start(bf16[64,32,8,128]{3,2,1,0:T(8,128)(2,1)} %bitcast.82), calls=%async_computation | async-start | bytes 8388608 | tf_op jit(solution)/shard_map/all_to_all | solution.py:82
  31.6 194.9 %copy-start.5 = (bf16[24,8,8,128]{3,2,1,0:T(8,128)(2,1)}, bf16[24,8,8,128]{3,2,1,0:T(8,128)(2,1)S(1)}, u32[]{:S(2)}) copy-start(bf16[24,8,8,128]{3,2,1,0:T(8,128)(2,1)S(1)} %copy.47) | copy-start | bytes 1179652
  219.0 9.9 %copy-start.2 = (bf16[128,1,8,8,128]{4,3,2,1,0:T(8,128)(2,1)}, bf16[128,1,8,8,128]{4,3,2,1,0:T(8,128)(2,1)S(1)}, u32[]{:S(2)}) copy-start(bf16[128,1,8,8,128]{4,3,2,1,0:T(8,128)(2,1)S(1)} %get-tuple-element.8) | copy-start | bytes 6291460
  219.0 12.2 %copy-start = (f32[128,1,8,8,128]{4,3,2,1,0:T(8,128)}, f32[128,1,8,8,128]{4,3,2,1,0:T(8,128)S(1)}, u32[]{:S(2)}) copy-start(f32[128,1,8,8,128]{4,3,2,1,0:T(8,128)S(1)} %get-tuple-element.9) | copy-start | bytes 12582916
  226.5 4.7 %copy-start.1 = (bf16[8,1024,192]{1,2,0:T(8,128)(2,1)}, bf16[8,1024,192]{1,2,0:T(8,128)(2,1)S(1)}, u32[]{:S(2)}) copy-start(bf16[8,1024,192]{1,2,0:T(8,128)(2,1)S(1)} %fusion.9) | copy-start | bytes 9437188
  235.7 16.8 %copy-start.7 = (s32[64,1]{0,1:T(1,128)S(1)}, s32[64,1]{0,1:T(1,128)}, u32[]{:S(2)}) copy-start(s32[64,1]{0,1:T(1,128)} %param.10) | copy-start | bytes 772
  237.4 121.8 %all-to-all-start.1 = ((bf16[64,18,8,128]{3,2,1,0:T(8,128)(2,1)}), bf16[64,18,8,128]{3,2,1,0:T(8,128)(2,1)}, u32[]{:S(2)}, u32[]{:S(2)}) async-start(bf16[64,18,8,128]{3,2,1,0:T(8,128)(2,1)} %pad_maximum_fusion), calls=%async_computation.1 | async-start | bytes 4718592 | tf_op jit(solution)/shard_map/all_to_all | solution.py:95
